TPU v7x, 512 devices: a whole 4x8x8 slice. The times are simulated.
512 devices in a mesh: fsdp: 128 (over y, z, core), tensor: 4 (over x).
Axes of the slice: x: 4, y: 8, z: 8, core: 2. Of those that a mesh axis runs over, the one named last changes fastest.
Arguments:
- layer_inputs: bfloat16 [2, 49152, 5120], P(None, 'fsdp', 'tensor'), may hold values from -8 to 8, as said below
- out_grads: bfloat16 [2, 49152, 2560], P(None, 'fsdp', 'tensor'), may hold values from -8 to 8, as said below
- weight_grad: bfloat16 [2, 2560, 5120], P(None, 'fsdp', 'tensor'), may hold values from -0.059814453 to 0.059814453
- emb_grad: bfloat16 [50176, 2560], P('fsdp', 'tensor'), may hold values from -0.59765625 to 0.59765625
- counts: int32 [50176], P('fsdp'), may hold values from 0 to 250
- owner_pos: int32 [4, 30], P('tensor'), may hold values from 0 to 127, as said below
Outputs:
- update: bfloat16 [2, 2560, 5120], P(None, 'fsdp', 'tensor')
- owner_inverses: float32 [4, 128, 128, 128], P('tensor', 'fsdp')
- emb_update: bfloat16 [50176, 2560], P('fsdp', 'tensor')
Inputs may be any that keep to these rules, and one draw needn't show every extreme that they name: `layer_inputs`: every element lies within the stated range; inner units in groups of four share a common part. `out_grads`: every element lies within the stated range; features in groups of four share a common part. `owner_pos`: the 30 entries of a row are distinct; slot p belongs to fsdp index p; some fsdp index holds 1 block of each row.
All inputs are finite; a program needn't handle non-finite values. Where the computation divides by a largest or mean magnitude, that divisor is 1e-20 or more.
Results may differ from a plain program's by a relative error of at most 0.0062.
Values may be sent and summed in bfloat16 or wider, within the bound.
No kernel may reach another device: no remote copies, remote signals or barrier semaphores. Data moves between devices by JAX's collectives and lax.ppermute only.
A program may use at most 64 MiB of HBM per device.

v0:
```python
import jax
import jax.numpy as jnp
from jax import lax
from jax.sharding import PartitionSpec as P

BLK = 128
NS_ITERS = 8


DAMP = 0.02
EDAMP = 0.25


def newton_inverse(factor):
    identity = jnp.eye(factor.shape[-1], dtype=jnp.float32)
    damped = factor + DAMP * identity
    norm_scale = jnp.max(jnp.sum(jnp.abs(damped), axis=-1), axis=-1)
    approx = identity[None] / norm_scale[:, None, None]
    for sweep_idx in range(NS_ITERS):
        product = jnp.einsum("bij,bjk->bik", damped, approx, precision=lax.Precision.HIGHEST)
        approx = jnp.einsum(
            "bij,bjk->bik", approx, 2.0 * identity[None] - product, precision=lax.Precision.HIGHEST
        )
    return approx


def on_device(layer_inputs, out_grads, weight_grad, emb_grad, counts, owner_pos):
    fsdp_size = lax.axis_size("fsdp")
    layers, row_count, inner_local = layer_inputs.shape
    width_local = out_grads.shape[2]
    a_count = inner_local // BLK
    g_count = width_local // BLK
    input_blocks = layer_inputs.reshape(layers, row_count, a_count, BLK)
    a_part = jnp.einsum(
        "lrbi,lrbj->lbij", input_blocks, input_blocks, preferred_element_type=jnp.float32
    )
    grad_blocks = out_grads.reshape(layers, row_count, g_count, BLK)
    g_part = jnp.einsum(
        "lrbi,lrbj->lbij", grad_blocks, grad_blocks, preferred_element_type=jnp.float32
    )
    partials = jnp.concatenate([a_part, g_part], axis=1)
    count_part = jnp.sum(counts.astype(jnp.float32))
    block_total = layers * (a_count + g_count)
    own_table = owner_pos[0]
    slot_count = (block_total + fsdp_size - 1) // fsdp_size
    wanted = lax.axis_index("fsdp") * slot_count + jnp.arange(slot_count, dtype=jnp.int32)
    one_hot = (own_table[None, :] == wanted[:, None]).astype(jnp.float32)
    divisor = row_count * fsdp_size
    summed, count_total = lax.psum((partials, count_part), "fsdp")
    factors = (summed / divisor).reshape(-1, BLK, BLK)
    mine_blocks = jnp.einsum("sk,kij->sij", one_hot, factors, precision=lax.Precision.HIGHEST)
    held_inv = newton_inverse(mine_blocks) * jnp.max(one_hot, axis=1)[:, None, None]
    owner_out = held_inv[None]
    shared = lax.all_gather(held_inv.astype(jnp.bfloat16), "fsdp", axis=0, tiled=True)
    low_inv = jnp.take(shared, own_table, axis=0)
    low_inv = low_inv.reshape(layers, a_count + g_count, BLK, BLK)
    a_low = low_inv[:, :a_count]
    g_own = low_inv[:, a_count:]
    g_all = lax.all_gather(g_own, "tensor", axis=1, tiled=True)
    d_local = weight_grad.shape[1]
    grad_split = weight_grad.reshape(layers, d_local, a_count, BLK)
    right_done = jnp.einsum(
        "ldbi,lbij->ldbj", grad_split, a_low, preferred_element_type=jnp.float32
    )
    right_done = right_done.reshape(layers, d_local, inner_local).astype(jnp.bfloat16)
    columns = lax.all_to_all(right_done, "fsdp", split_axis=2, concat_axis=1, tiled=True)
    full_width = columns.shape[1]
    column_blocks = columns.reshape(layers, full_width // BLK, BLK, columns.shape[2])
    left_done = jnp.einsum(
        "lbij,lbjc->lbic", g_all, column_blocks, preferred_element_type=jnp.float32
    )
    left_done = left_done.reshape(columns.shape).astype(jnp.bfloat16)
    update = lax.all_to_all(left_done, "fsdp", split_axis=1, concat_axis=2, tiled=True)
    vocab_total = counts.shape[0] * fsdp_size
    frequency = counts.astype(jnp.float32) * vocab_total / count_total
    emb_update = (emb_grad.astype(jnp.float32) / (frequency + EDAMP)[:, None]).astype(jnp.bfloat16)
    return (update, owner_out, emb_update)


def solution(mesh):
    placed = (
        P(None, "fsdp", "tensor"),
        P(None, "fsdp", "tensor"),
        P(None, "fsdp", "tensor"),
        P("fsdp", "tensor"),
        P("fsdp"),
        P("tensor", None),
    )
    return jax.shard_map(
        on_device,
        mesh=mesh,
        in_specs=placed,
        out_specs=(P(None, "fsdp", "tensor"), P("tensor", "fsdp", None, None), P("fsdp", "tensor")),
        check_vma=False,
    )
```

profile of v0, /device:TPU:1, one launch (start us, length us, event | category | flops | bytes accessed | tf_op | source)
XLA Modules:
  0.0 627.3 jit_solution(3849056643370400006)
XLA Ops:
  7.2 2.8 copy.41
  10.1 0.9 fusion.20
  11.0 1.6 copy.43
  13.1 1.4 pad_maximum_fusion
  15.2 0.6 fusion.14
  15.8 206.1 %all-reduce.2.cloned.1.call-done = f32[2,15,128,128]{3,2,1,0:T(8,128)} async-done(((f32[2,15,128,128]{3,2,1,0:T(8,128)}), f32[2,15,128,128]{3,2,1,0:T(8,128)}) %all-reduce.2.cloned.1.call-update) | async-done | bytes 1966096 | tf_op jit(solution)/shard_map/psum | solution.py:49
  221.9 1.7 broadcast_multiply_fusion
  223.6 1.9 fusion
  225.6 0.6 reduce_max.18
  230.1 1.5 fusion.19
  232.2 0.7 reduce.8
  232.9 81.3 %all-gather.6.cloned.1.call-done = bf16[16384,128]{1,0:T(8,128)(2,1)} async-done(((bf16[128,128]{1,0:T(8,128)(2,1)}), bf16[16384,128]{1,0:T(8,128)(2,1)}) %all-gather.6.cloned.1.call-update) | async-done | bytes 4194320 | tf_op jit(solution)/shard_map/all_gather | solution.py:54
  314.3 2.9 gather_fusion
  317.4 0.7 slice.10
  318.2 0.6 convert_reduce_fusion
  318.8 247.1 %psum.15 = f32[]{:T(128)} all-reduce(f32[]{:T(128)} %convert_reduce_fusion), channel_id=1, replica_groups=mesh['fsdp'=128,'tensor'=4] {'fsdp'}, use_global_device_ids=true, to_apply=%region_5.0 | all-reduce | flops 1 | bytes 8 | tf_op jit(solution)/shard_map/psum | solution.py:49
  566.7 1.2 reshape.204
  567.9 10.2 %all-to-all-start = ((bf16[128,2,200]{2,1,0:T(2,128)(2,1)}), bf16[128,2,200]{2,1,0:T(2,128)(2,1)S(1)}, u32[]{:S(2)}, u32[]{:S(2)}) async-start(bf16[128,2,200]{2,1,0:T(2,128)(2,1)} %reshape.204), calls=%async_computation | async-start | bytes 262144 | tf_op jit(solution)/shard_map/all_to_all | solution.py:66
  578.1 0.7 divide_add_fusion
  578.7 11.6 %all-to-all-done = bf16[128,2,200]{2,1,0:T(2,128)(2,1)S(1)} async-done(((bf16[128,2,200]{2,1,0:T(2,128)(2,1)}), bf16[128,2,200]{2,1,0:T(2,128)(2,1)S(1)}, u32[]{:S(2)}, u32[]{:S(2)}) %all-to-all-start) | async-done | bytes 102432 | tf_op jit(solution)/shard_map/all_to_all | solution.py:66
  590.3 0.6 reshape.205
  591.1 1.4 reshape.183
  592.5 2.1 convolution_convert_fusion
  594.5 1.1 copy.60
  595.6 1.6 reshape.206
  597.2 6.1 all-to-all-start.1
  603.4 1.0 divide_convert_fusion
  604.3 11.4 %all-to-all-done.1 = bf16[128,2,200]{2,1,0:T(2,128)(2,1)S(1)} async-done(((bf16[128,2,200]{2,1,0:T(2,128)(2,1)}), bf16[128,2,200]{2,1,0:T(2,128)(2,1)S(1)}, u32[]{:S(2)}, u32[]{:S(2)}) %all-to-all-start.1) | async-done | bytes 102432 | tf_op jit(solution)/shard_map/all_to_all | solution.py:73
  615.7 1.0 reshape.207
  616.7 2.3 copy.61
  619.0 0.7 copy.53
  619.7 1.1 copy.54
  (42 shorter events, 6.3 us)
Async XLA Ops:
  7.2 214.7 %all-reduce.2.cloned.1.call-start = ((), (), s32[]{:S(2)}) async-start(), calls=%async_computation.2 | async-start | bytes 3932160 | tf_op jit(solution)/shard_map/psum | solution.py:49
  14.6 0.7 copy-start.3
  14.6 299.7 %all-gather.6.cloned.1.call-start = ((), (), s32[]{:S(2)}) async-start(), calls=%async_computation.4 | async-start | bytes 4227072 | tf_op jit(solution)/shard_map/all_gather | solution.py:54
  231.6 360.8 %all-gather.4.cloned.1.call-start = ((), (), s32[]{:S(2)}) async-start(), calls=%async_computation.3 | async-start | bytes 1638400 | tf_op jit(solution)/shard_map/all_gather | solution.py:59
  317.2 1.0 copy-start.2
  317.2 248.6 %copy-start.1 = (bf16[2,20,1280]{2,0,1:T(2,128)(2,1)S(1)}, bf16[2,20,1280]{2,0,1:T(2,128)(2,1)}, u32[]{:S(2)}) copy-start(bf16[2,20,1280]{2,0,1:T(2,128)(2,1)} %param.8) | copy-start | bytes 307204
  567.9 22.4 %all-to-all-start = ((bf16[128,2,200]{2,1,0:T(2,128)(2,1)}), bf16[128,2,200]{2,1,0:T(2,128)(2,1)S(1)}, u32[]{:S(2)}, u32[]{:S(2)}) async-start(bf16[128,2,200]{2,1,0:T(2,128)(2,1)} %reshape.204), calls=%async_computation | async-start | bytes 262144 | tf_op jit(solution)/shard_map/all_to_all | solution.py:66
  594.5 8.8 %copy-start = (bf16[392,640]{1,0:T(8,128)(2,1)S(1)}, bf16[392,640]{1,0:T(8,128)(2,1)}, u32[]{:S(2)}) copy-start(bf16[392,640]{1,0:T(8,128)(2,1)} %param.9) | copy-start | bytes 1505284
  597.2 18.5 %all-to-all-start.1 = ((bf16[128,2,200]{2,1,0:T(2,128)(2,1)}), bf16[128,2,200]{2,1,0:T(2,128)(2,1)S(1)}, u32[]{:S(2)}, u32[]{:S(2)}) async-start(bf16[128,2,200]{2,1,0:T(2,128)(2,1)} %reshape.206), calls=%async_computation.1 | async-start | bytes 262144 | tf_op jit(solution)/shard_map/all_to_all | solution.py:73
Sparse Core Ops, SparseCore 0:
  14.7 207.1 all-reduce.1
  231.7 82.4 all-gather.5
  318.3 25.3 all-gather.3
where the time goes:
time: 628 us; the launch traced here: 627 us
  waiting for transfers between devices  310 us (49%)
  blocking collectives  247 us (39%)
  local copies, waits for them, and re-layouts  20.9 us (3%)
  starting transfers between devices  16.4 us (3%)
  between operations  14.8 us (2%)
  matrix products  10.3 us (2%)
  other arithmetic  7.5 us (1%)
    psum x1, blocking collectives, on_device(): summed, count_total = lax.psum((partials, count_part), 'fsdp')  247 us
    psum x1, waiting for transfers between devices, on_device(): summed, count_total = lax.psum((partials, count_part), 'fsdp')  206 us
    all_gather x1, waiting for transfers between devices, on_device(): lax.all_gather(held_inv.astype(jnp.bfloat16), 'fsdp', axis=0, tiled=True)  81.3 us
  transfers between devices with their start and end apart: 5, of which 4 were waited for; matrix products, arithmetic and copies ran while one was open for 1% of the time, Pallas kernels for 0%

commit v1 on v0

--- a/solution.py
+++ b/solution.py
@@ -16,12 +16,14 @@
     damped = factor + DAMP * identity
     norm_scale = jnp.max(jnp.sum(jnp.abs(damped), axis=-1), axis=-1)
     approx = identity[None] / norm_scale[:, None, None]
-    for sweep_idx in range(NS_ITERS):
+
+    def sweep(sweep_idx, approx):
         product = jnp.einsum("bij,bjk->bik", damped, approx, precision=lax.Precision.HIGHEST)
-        approx = jnp.einsum(
+        return jnp.einsum(
             "bij,bjk->bik", approx, 2.0 * identity[None] - product, precision=lax.Precision.HIGHEST
         )
-    return approx
+
+    return lax.fori_loop(0, NS_ITERS, sweep, approx)
 
 
 def on_device(layer_inputs, out_grads, weight_grad, emb_grad, counts, owner_pos):
@@ -38,22 +40,23 @@
     g_part = jnp.einsum(
         "lrbi,lrbj->lbij", grad_blocks, grad_blocks, preferred_element_type=jnp.float32
     )
-    partials = jnp.concatenate([a_part, g_part], axis=1)
+    block_total = layers * (a_count + g_count)
+    partials = jnp.concatenate([a_part, g_part], axis=1).reshape(block_total * BLK, BLK)
     count_part = jnp.sum(counts.astype(jnp.float32))
-    block_total = layers * (a_count + g_count)
+    count_rows = jnp.zeros((8, BLK), jnp.float32).at[0, 0].set(count_part)
+    packed = jnp.concatenate([partials, count_rows], axis=0)
+    summed = lax.psum(packed, "fsdp")
+    count_total = summed[block_total * BLK, 0]
+    divisor = row_count * fsdp_size
+    factors = (summed[: block_total * BLK] / divisor).reshape(block_total, BLK, BLK)
+    inv = newton_inverse(factors)
     own_table = owner_pos[0]
-    slot_count = (block_total + fsdp_size - 1) // fsdp_size
-    wanted = lax.axis_index("fsdp") * slot_count + jnp.arange(slot_count, dtype=jnp.int32)
-    one_hot = (own_table[None, :] == wanted[:, None]).astype(jnp.float32)
-    divisor = row_count * fsdp_size
-    summed, count_total = lax.psum((partials, count_part), "fsdp")
-    factors = (summed / divisor).reshape(-1, BLK, BLK)
-    mine_blocks = jnp.einsum("sk,kij->sij", one_hot, factors, precision=lax.Precision.HIGHEST)
-    held_inv = newton_inverse(mine_blocks) * jnp.max(one_hot, axis=1)[:, None, None]
-    owner_out = held_inv[None]
-    shared = lax.all_gather(held_inv.astype(jnp.bfloat16), "fsdp", axis=0, tiled=True)
-    low_inv = jnp.take(shared, own_table, axis=0)
-    low_inv = low_inv.reshape(layers, a_count + g_count, BLK, BLK)
+    slot = lax.axis_index("fsdp")
+    hit = own_table == slot
+    pick = jnp.argmax(hit)
+    held = lax.dynamic_index_in_dim(inv, pick, axis=0, keepdims=True)
+    owner_out = jnp.where(jnp.any(hit), held, 0.0)[None]
+    low_inv = inv.astype(jnp.bfloat16).reshape(layers, a_count + g_count, BLK, BLK)
     a_low = low_inv[:, :a_count]
     g_own = low_inv[:, a_count:]
     g_all = lax.all_gather(g_own, "tensor", axis=1, tiled=True)

time: 628 us -> 376 us (0.60)
  blocking collectives: 247 us -> 0 us
  waiting for transfers between devices: 310 us -> 226 us
  matrix products: 10.3 us -> 64.7 us
  local copies, waits for them, and re-layouts: 20.9 us -> 34.3 us
    psum x1 -> x0, blocking collectives: 247 us -> none  [on_device(): summed, count_total = lax.psum((partials, count_part), 'fsdp')]
    all_gather x1 -> x0, waiting for transfers between devices: 81.3 us -> none  [on_device(): lax.all_gather(held_inv.astype(jnp.bfloat16), 'fsdp', axis=0, tiled=True)]
    dot_general x17 -> x16, matrix products: 6.44 us -> 60.7 us  [the longest x8 33.8 us: sweep(): jnp.einsum('bij,bjk->bik', damped, approx, precision=lax.Precision.HIGHEST)]
    while x0 -> x25, local copies, waits for them, and re-layouts: none -> 13.9 us
  transfers between devices with their start and end apart: 5 -> 4, of which waited for: 4 -> 3; matrix products, arithmetic and copies ran while one was open for 1% -> 3% of each run, Pallas kernels for 0% -> 0%
where the time goes in v1:
time: 376 us; the launch traced here: 375 us
  waiting for transfers between devices  226 us (60%)
  matrix products  64.7 us (17%)
  local copies, waits for them, and re-layouts  34.3 us (9%)
  starting transfers between devices  20.9 us (6%)
  between operations  16.2 us (4%)
  other arithmetic  12.7 us (3%)
    psum x1, waiting for transfers between devices, on_device(): summed = lax.psum(packed, 'fsdp')  207 us
    dot_general x8, matrix products, sweep(): jnp.einsum('bij,bjk->bik', damped, approx, precision=lax.Precision.HIGHEST)  33.8 us
    dot_general x8, matrix products, sweep(): jnp.einsum('bij,bjk->bik', approx, 2.0 * identity[None] - product, precis...  26.9 us
    while x24, local copies, waits for them, and re-layouts  12.1 us
    all_to_all x1, waiting for transfers between devices, on_device(): lax.all_to_all(left_done, 'fsdp', split_axis=1, concat_axis=2, tiled=True)  11.3 us
    all_to_all x1, starting transfers between devices, on_device(): lax.all_to_all(right_done, 'fsdp', split_axis=2, concat_axis=1, tiled=True)  11.1 us
    unnamed x15, local copies, waits for them, and re-layouts  9.88 us
    all_to_all x1, starting transfers between devices, on_device(): lax.all_to_all(left_done, 'fsdp', split_axis=1, concat_axis=2, tiled=True)  9.69 us
  transfers between devices with their start and end apart: 4, of which 3 were waited for; matrix products, arithmetic and copies ran while one was open for 3% of the time, Pallas kernels for 0%

profile of v1, /device:TPU:1, one launch (start us, length us, event | category | flops | bytes accessed | tf_op | source)
XLA Modules:
  0.0 375.5 jit_solution(11670501787873798330)
XLA Ops:
  8.5 1.6 copy.81
  10.6 2.8 copy.79
  14.6 2.0 select_maximum_fusion
  16.8 206.8 %all-reduce.3.cloned.1.call-done = f32[3848,128]{1,0:T(8,128)} async-done(((f32[3848,128]{1,0:T(8,128)}), f32[3848,128]{1,0:T(8,128)}) %all-reduce.3.cloned.1.call-update) | async-done | bytes 1970192 | tf_op jit(solution)/shard_map/psum | solution.py:48
  223.6 2.1 slice_multiply_fusion
  227.6 73.2 %while.12 = (s32[]{:T(128)}, f32[30,128,128]{1,2,0:T(8,128)S(1)}, f32[30,128,128]{2,1,0:T(8,128)}, s32[]{:T(128)}) while((s32[]{:T(128)}, f32[30,128,128]{1,2,0:T(8,128)S(1)}, f32[30,128,128]{2,1,0:T(8,128)}, s32[]{:T(128)}) %tuple.36), condition=%wide.region_5.0_spmd.clone, body=%wide.region_4.0_spmd.clone.sunk | while | flops 1510473728 | bytes 23724112 | solution.py:26
  229.1 4.2 %fusion.39 = f32[30,128,128]{2,1,0:T(8,128)S(1)} fusion(f32[30,128,128]{2,1,0:T(8,128)S(1)} %copy-done, f32[30,128,128]{1,2,0:T(8,128)S(1)} %copy.117), kind=kOutput, calls=%fused_computation.31.clone.1 | convolution fusion | flops 754974720 | bytes 5898240 | tf_op jit(solution)/shard_map/while/body/eval_jaxpr/bij,bjk->bik/dot_general | solution.py:21
  233.4 3.4 fusion.41
  238.3 4.2 %fusion.39 = f32[30,128,128]{2,1,0:T(8,128)S(1)} fusion(f32[30,128,128]{2,1,0:T(8,128)S(1)} %copy-done, f32[30,128,128]{1,2,0:T(8,128)S(1)} %copy.117), kind=kOutput, calls=%fused_computation.31.clone.1 | convolution fusion | flops 754974720 | bytes 5898240 | tf_op jit(solution)/shard_map/while/body/eval_jaxpr/bij,bjk->bik/dot_general | solution.py:21
  242.5 3.4 fusion.41
  247.4 4.2 %fusion.39 = f32[30,128,128]{2,1,0:T(8,128)S(1)} fusion(f32[30,128,128]{2,1,0:T(8,128)S(1)} %copy-done, f32[30,128,128]{1,2,0:T(8,128)S(1)} %copy.117), kind=kOutput, calls=%fused_computation.31.clone.1 | convolution fusion | flops 754974720 | bytes 5898240 | tf_op jit(solution)/shard_map/while/body/eval_jaxpr/bij,bjk->bik/dot_general | solution.py:21
  251.7 3.4 fusion.41
  256.6 4.2 %fusion.39 = f32[30,128,128]{2,1,0:T(8,128)S(1)} fusion(f32[30,128,128]{2,1,0:T(8,128)S(1)} %copy-done, f32[30,128,128]{1,2,0:T(8,128)S(1)} %copy.117), kind=kOutput, calls=%fused_computation.31.clone.1 | convolution fusion | flops 754974720 | bytes 5898240 | tf_op jit(solution)/shard_map/while/body/eval_jaxpr/bij,bjk->bik/dot_general | solution.py:21
  260.8 3.4 fusion.41
  265.7 4.2 %fusion.39 = f32[30,128,128]{2,1,0:T(8,128)S(1)} fusion(f32[30,128,128]{2,1,0:T(8,128)S(1)} %copy-done, f32[30,128,128]{1,2,0:T(8,128)S(1)} %copy.117), kind=kOutput, calls=%fused_computation.31.clone.1 | convolution fusion | flops 754974720 | bytes 5898240 | tf_op jit(solution)/shard_map/while/body/eval_jaxpr/bij,bjk->bik/dot_general | solution.py:21
  270.0 3.4 fusion.41
  274.9 4.2 %fusion.39 = f32[30,128,128]{2,1,0:T(8,128)S(1)} fusion(f32[30,128,128]{2,1,0:T(8,128)S(1)} %copy-done, f32[30,128,128]{1,2,0:T(8,128)S(1)} %copy.117), kind=kOutput, calls=%fused_computation.31.clone.1 | convolution fusion | flops 754974720 | bytes 5898240 | tf_op jit(solution)/shard_map/while/body/eval_jaxpr/bij,bjk->bik/dot_general | solution.py:21
  279.1 3.4 fusion.41
  284.1 4.2 %fusion.39 = f32[30,128,128]{2,1,0:T(8,128)S(1)} fusion(f32[30,128,128]{2,1,0:T(8,128)S(1)} %copy-done, f32[30,128,128]{1,2,0:T(8,128)S(1)} %copy.117), kind=kOutput, calls=%fused_computation.31.clone.1 | convolution fusion | flops 754974720 | bytes 5898240 | tf_op jit(solution)/shard_map/while/body/eval_jaxpr/bij,bjk->bik/dot_general | solution.py:21
  288.3 3.4 fusion.41
  293.2 4.2 %fusion.39 = f32[30,128,128]{2,1,0:T(8,128)S(1)} fusion(f32[30,128,128]{2,1,0:T(8,128)S(1)} %copy-done, f32[30,128,128]{1,2,0:T(8,128)S(1)} %copy.117), kind=kOutput, calls=%fused_computation.31.clone.1 | convolution fusion | flops 754974720 | bytes 5898240 | tf_op jit(solution)/shard_map/while/body/eval_jaxpr/bij,bjk->bik/dot_general | solution.py:21
  297.4 3.4 fusion.41
  302.3 1.7 slice.33
  307.4 1.8 copy.93
  311.3 11.1 %all-to-all-start = ((bf16[128,2,200]{2,1,0:T(2,128)(2,1)}), bf16[128,2,200]{2,1,0:T(2,128)(2,1)S(1)}, u32[]{:S(2)}, u32[]{:S(2)}) async-start(bf16[128,2,200]{2,1,0:T(2,128)(2,1)} %reshape.95), calls=%async_computation | async-start | bytes 262144 | tf_op jit(solution)/shard_map/all_to_all | solution.py:69
  323.7 2.1 select_bitcast_fusion
  326.6 8.2 %all-to-all-done = bf16[128,2,200]{2,1,0:T(2,128)(2,1)S(1)} async-done(((bf16[128,2,200]{2,1,0:T(2,128)(2,1)}), bf16[128,2,200]{2,1,0:T(2,128)(2,1)S(1)}, u32[]{:S(2)}, u32[]{:S(2)}) %all-to-all-start) | async-done | bytes 102432 | tf_op jit(solution)/shard_map/all_to_all | solution.py:69
  336.8 2.1 convolution_convert_fusion
  340.0 1.6 reshape.97
  341.6 9.7 %all-to-all-start.1 = ((bf16[128,2,200]{2,1,0:T(2,128)(2,1)}), bf16[128,2,200]{2,1,0:T(2,128)(2,1)S(1)}, u32[]{:S(2)}, u32[]{:S(2)}) async-start(bf16[128,2,200]{2,1,0:T(2,128)(2,1)} %reshape.97), calls=%async_computation.1 | async-start | bytes 262144 | tf_op jit(solution)/shard_map/all_to_all | solution.py:76
  352.3 11.3 %all-to-all-done.1 = bf16[128,2,200]{2,1,0:T(2,128)(2,1)S(1)} async-done(((bf16[128,2,200]{2,1,0:T(2,128)(2,1)}), bf16[128,2,200]{2,1,0:T(2,128)(2,1)S(1)}, u32[]{:S(2)}, u32[]{:S(2)}) %all-to-all-start.1) | async-done | bytes 102432 | tf_op jit(solution)/shard_map/all_to_all | solution.py:76
  364.5 2.3 copy.102
  (73 shorter events, 30.9 us)
Async XLA Ops:
  7.2 216.5 %all-reduce.3.cloned.1.call-start = ((), (), s32[]{:S(2)}) async-start(), calls=%async_computation.2 | async-start | bytes 3940352 | tf_op jit(solution)/shard_map/psum | solution.py:48
  16.7 320.2 %all-gather.2.cloned.1.call-start = ((), (), s32[]{:S(2)}) async-start(), calls=%async_computation.3 | async-start | bytes 1638400 | tf_op jit(solution)/shard_map/all_gather | solution.py:62
  227.6 1.5 copy-start
  236.7 1.5 copy-start
  245.9 1.5 copy-start
  255.0 1.5 copy-start
  264.2 1.5 copy-start
  273.4 1.5 copy-start
  282.5 1.5 copy-start
  291.7 1.5 copy-start
  301.0 3.1 copy-start.4
  301.0 5.0 %copy-start.2 = (bf16[2,20,1280]{2,0,1:T(2,128)(2,1)S(1)}, bf16[2,20,1280]{2,0,1:T(2,128)(2,1)}, u32[]{:S(2)}) copy-start(bf16[2,20,1280]{2,0,1:T(2,128)(2,1)} %param.12) | copy-start | bytes 307204
  309.1 16.7 %copy-start.3 = (s32[392]{0:T(512)S(1)}, s32[392]{0:T(512)}, u32[]{:S(2)}) copy-start(s32[392]{0:T(512)} %param.14) | copy-start | bytes 4708
  311.3 23.4 %all-to-all-start = ((bf16[128,2,200]{2,1,0:T(2,128)(2,1)}), bf16[128,2,200]{2,1,0:T(2,128)(2,1)S(1)}, u32[]{:S(2)}, u32[]{:S(2)}) async-start(bf16[128,2,200]{2,1,0:T(2,128)(2,1)} %reshape.95), calls=%async_computation | async-start | bytes 262144 | tf_op jit(solution)/shard_map/all_to_all | solution.py:69
  338.9 12.4 %copy-start.1 = (bf16[392,640]{1,0:T(8,128)(2,1)S(1)}, bf16[392,640]{1,0:T(8,128)(2,1)}, u32[]{:S(2)}) copy-start(bf16[392,640]{1,0:T(8,128)(2,1)} %param.13) | copy-start | bytes 1505284
  341.6 22.0 %all-to-all-start.1 = ((bf16[128,2,200]{2,1,0:T(2,128)(2,1)}), bf16[128,2,200]{2,1,0:T(2,128)(2,1)S(1)}, u32[]{:S(2)}, u32[]{:S(2)}) async-start(bf16[128,2,200]{2,1,0:T(2,128)(2,1)} %reshape.97), calls=%async_computation.1 | async-start | bytes 262144 | tf_op jit(solution)/shard_map/all_to_all | solution.py:76
Sparse Core Ops, SparseCore 0:
  16.8 206.8 all-reduce.2
  304.1 26.9 all-gather.1

commit v2 on v1

--- a/solution.py
+++ b/solution.py
@@ -26,6 +26,48 @@
     return lax.fori_loop(0, NS_ITERS, sweep, approx)
 
 
+def pack_symmetric(blocks, count_part, fsdp_size):
+    half = BLK // 2
+    rows = lax.broadcasted_iota(jnp.int32, (half, half), 0)
+    cols = lax.broadcasted_iota(jnp.int32, (half, half), 1)
+    upper_left = blocks[:, :half, :half]
+    lower_right = jnp.flip(blocks[:, half:, half:], (1, 2))
+    folded = jnp.where(rows < cols, upper_left, lower_right)
+    panel = jnp.concatenate([folded, blocks[:, :half, half:]], axis=2)
+    diag = jnp.diagonal(upper_left, axis1=1, axis2=2).reshape(-1, BLK)
+    count_row = jnp.zeros((1, BLK), jnp.float32).at[0, 0].set(count_part)
+    body = jnp.concatenate([panel.reshape(-1, BLK), diag, count_row], axis=0)
+    total = -(-body.shape[0] // fsdp_size) * fsdp_size
+    return jnp.concatenate([body, jnp.zeros((total - body.shape[0], BLK), jnp.float32)], axis=0)
+
+
+def unpack_symmetric(summed, block_total):
+    half = BLK // 2
+    panel = summed[: block_total * half].reshape(block_total, half, BLK)
+    diag_rows = block_total * half // BLK
+    diag = summed[block_total * half : block_total * half + diag_rows].reshape(block_total, half)
+    count_total = summed[block_total * half + diag_rows, 0]
+    rows = lax.broadcasted_iota(jnp.int32, (half, half), 0)
+    cols = lax.broadcasted_iota(jnp.int32, (half, half), 1)
+    folded = panel[:, :, :half]
+    upper_right = panel[:, :, half:]
+    folded_t = jnp.swapaxes(folded, 1, 2)
+    upper_left = jnp.where(rows < cols, folded, jnp.where(rows > cols, folded_t, diag[:, :, None]))
+    turned = jnp.flip(folded, (1, 2))
+    lower_right = jnp.where(rows <= cols, turned, jnp.swapaxes(turned, 1, 2))
+    top = jnp.concatenate([upper_left, upper_right], axis=2)
+    bottom = jnp.concatenate([jnp.swapaxes(upper_right, 1, 2), lower_right], axis=2)
+    return jnp.concatenate([top, bottom], axis=1), count_total
+
+
+def sum_over_fsdp(packed, fsdp_size):
+    chunk = packed.shape[0] // fsdp_size
+    pieces = lax.all_to_all(packed.reshape(fsdp_size, chunk, BLK), "fsdp", 0, 0, tiled=True)
+    mine = jnp.sum(pieces, axis=0)
+    spread = jnp.broadcast_to(mine[None], (fsdp_size, chunk, BLK))
+    return lax.all_to_all(spread, "fsdp", 0, 0, tiled=True).reshape(packed.shape)
+
+
 def on_device(layer_inputs, out_grads, weight_grad, emb_grad, counts, owner_pos):
     fsdp_size = lax.axis_size("fsdp")
     layers, row_count, inner_local = layer_inputs.shape
@@ -41,14 +83,13 @@
         "lrbi,lrbj->lbij", grad_blocks, grad_blocks, preferred_element_type=jnp.float32
     )
     block_total = layers * (a_count + g_count)
-    partials = jnp.concatenate([a_part, g_part], axis=1).reshape(block_total * BLK, BLK)
+    partials = jnp.concatenate([a_part, g_part], axis=1).reshape(block_total, BLK, BLK)
     count_part = jnp.sum(counts.astype(jnp.float32))
-    count_rows = jnp.zeros((8, BLK), jnp.float32).at[0, 0].set(count_part)
-    packed = jnp.concatenate([partials, count_rows], axis=0)
-    summed = lax.psum(packed, "fsdp")
-    count_total = summed[block_total * BLK, 0]
+    packed = pack_symmetric(partials, count_part, fsdp_size)
+    summed = sum_over_fsdp(packed, fsdp_size)
+    blocks_sum, count_total = unpack_symmetric(summed, block_total)
     divisor = row_count * fsdp_size
-    factors = (summed[: block_total * BLK] / divisor).reshape(block_total, BLK, BLK)
+    factors = blocks_sum / divisor
     inv = newton_inverse(factors)
     own_table = owner_pos[0]
     slot = lax.axis_index("fsdp")

time: 376 us -> 299 us (0.80)
  waiting for transfers between devices: 226 us -> 51.1 us
  blocking collectives: 0 us -> 48.7 us
  local copies, waits for them, and re-layouts: 34.3 us -> 68.5 us
  other arithmetic: 12.7 us -> 23.8 us
    psum x1 -> x0, waiting for transfers between devices: 207 us -> none  [on_device(): summed = lax.psum(packed, 'fsdp')]
    all_to_all x0 -> x1, blocking collectives: none -> 48.7 us  [sum_over_fsdp(): lax.all_to_all(packed.reshape(fsdp_size, chunk, BLK), 'fsdp', 0, 0, tiled...]
    all_to_all x0 -> x1, waiting for transfers between devices: none -> 30.1 us  [sum_over_fsdp(): lax.all_to_all(spread, 'fsdp', 0, 0, tiled=True).reshape(packed.shape)]
    select_n x0 -> x3, other arithmetic: none -> 12.6 us  [the longest x1 4.76 us: unpack_symmetric(): jnp.where(rows < cols, folded, jnp.where(rows > cols, folded_t, diag[:, :...]
    select_n x0 -> x3, local copies, waits for them, and re-layouts: none -> 9.19 us  [the longest x1 3.99 us: unpack_symmetric(): lower_right = jnp.where(rows <= cols, turned, jnp.swapaxes(turned, 1, 2))]
    unnamed x15 -> x26, local copies, waits for them, and re-layouts: 9.88 us -> 18.1 us
    rev x0 -> x2, local copies, waits for them, and re-layouts: none -> 7.59 us  [the longest x1 3.8 us: unpack_symmetric(): turned = jnp.flip(folded, (1, 2))]
    all_to_all x0 -> x1, starting transfers between devices: none -> 6.99 us  [sum_over_fsdp(): lax.all_to_all(spread, 'fsdp', 0, 0, tiled=True).reshape(packed.shape)]
  transfers between devices with their start and end apart: 4 -> 4, of which waited for: 3 -> 3; matrix products, arithmetic and copies ran while one was open for 3% -> 4% of each run, Pallas kernels for 0% -> 0%
where the time goes in v2:
time: 299 us; the launch traced here: 298 us
  local copies, waits for them, and re-layouts  68.5 us (23%)
  matrix products  64.7 us (22%)
  waiting for transfers between devices  51.1 us (17%)
  blocking collectives  48.7 us (16%)
  other arithmetic  23.8 us (8%)
  starting transfers between devices  22.8 us (8%)
  between operations  17.6 us (6%)
    all_to_all x1, blocking collectives, sum_over_fsdp(): lax.all_to_all(packed.reshape(fsdp_size, chunk, BLK), 'fsdp', 0, 0, tiled...  48.7 us
    dot_general x8, matrix products, sweep(): jnp.einsum('bij,bjk->bik', damped, approx, precision=lax.Precision.HIGHEST)  33.8 us
    all_to_all x1, waiting for transfers between devices, sum_over_fsdp(): lax.all_to_all(spread, 'fsdp', 0, 0, tiled=True).reshape(packed.shape)  30.1 us
    dot_general x8, matrix products, sweep(): jnp.einsum('bij,bjk->bik', approx, 2.0 * identity[None] - product, precis...  26.9 us
    unnamed x26, local copies, waits for them, and re-layouts  18.1 us
    while x24, local copies, waits for them, and re-layouts  12.1 us
    all_to_all x1, waiting for transfers between devices, on_device(): lax.all_to_all(left_done, 'fsdp', split_axis=1, concat_axis=2, tiled=True)  11.3 us
    all_to_all x1, waiting for transfers between devices, on_device(): lax.all_to_all(right_done, 'fsdp', split_axis=2, concat_axis=1, tiled=True)  9.61 us
  transfers between devices with their start and end apart: 4, of which 3 were waited for; matrix products, arithmetic and copies ran while one was open for 4% of the time, Pallas kernels for 0%

profile of v2, /device:TPU:1, one launch (start us, length us, event | category | flops | bytes accessed | tf_op | source)
XLA Modules:
  0.0 297.5 jit_solution(15386533167699822764)
XLA Ops:
  18.4 3.2 %copy.131 = f32[30,64,64]{0,2,1:T(8,128)} copy(f32[30,64,64]{2,1,0:T(8,128)} %get-tuple-element.71) | data formatting | bytes 983040
  21.6 3.8 %rev.7 = f32[30,64,64]{0,2,1:T(8,128)} reverse(f32[30,64,64]{0,2,1:T(8,128)} %copy.131), dimensions={1,2} | reverse | bytes 983040 | tf_op jit(solution)/shard_map/jit(_flip)/rev | solution.py:34
  28.9 3.6 %broadcast_select_fusion = f32[30,64,64]{0,2,1:T(8,128)} fusion(f32[30,64,64]{0,2,1:T(8,128)} %copy.130, f32[30,64,64]{0,2,1:T(8,128)} %rev.7, pred[64,64]{1,0:T(8,128)(4,1)S(1)} %get-tuple-element.78), kind=kLoop, calls=%fused_computation.18 | loop fusion | flops 122880 | bytes 1478656 | tf_op jit(solution)/shard_map/jit(_where)/select_n | solution.py:35
  35.8 48.7 %all_to_all.43 = f32[128,16,128]{2,1,0:T(8,128)S(1)} all-to-all(f32[128,16,128]{2,1,0:T(8,128)S(1)} %bitcast.72), channel_id=1, replica_groups=mesh['fsdp'=128,'tensor'=4] {'fsdp'}, dimensions={0} | all-to-all | bytes 2097152 | tf_op jit(solution)/shard_map/all_to_all | solution.py:65
  85.7 7.0 %all-to-all-start.1 = ((f32[128,16,128]{2,1,0:T(8,128)}), f32[128,16,128]{2,1,0:T(8,128)S(1)}, u32[]{:S(2)}, u32[]{:S(2)}) async-start(f32[128,16,128]{2,1,0:T(8,128)} %broadcast_in_dim.50), calls=%async_computation.1 | async-start | bytes 2097152 | tf_op jit(solution)/shard_map/all_to_all | solution.py:68
  93.1 30.1 %all-to-all-done.1 = f32[128,16,128]{2,1,0:T(8,128)S(1)} async-done(((f32[128,16,128]{2,1,0:T(8,128)}), f32[128,16,128]{2,1,0:T(8,128)S(1)}, u32[]{:S(2)}, u32[]{:S(2)}) %all-to-all-start.1) | async-done | bytes 1048608 | tf_op jit(solution)/shard_map/all_to_all | solution.py:68
  130.6 3.8 %rev.8 = f32[30,64,64]{0,1,2:T(8,128)} reverse(f32[30,64,64]{0,1,2:T(8,128)} %copy.132), dimensions={1,2} | reverse | bytes 983040 | tf_op jit(solution)/shard_map/jit(_flip)/rev | solution.py:56
  134.4 4.8 %fusion.9 = f32[30,64,64]{0,2,1:T(8,128)} fusion(f32[30,64,64]{0,2,1:T(8,128)} %copy.100, f32[30,64,64]{0,1,2:T(8,128)} %copy.132, f32[30,64]{0,1:T(8,128)S(1)} %copy.99, pred[64,64]{1,0:T(8,128)(4,1)S(1)} %get-tuple-element.77, pred[64,64]{1,0:T(8,128)(4,1)S(1)} %get-tuple-element.78), kind=kLoop, calls=%fused_computation.10 | loop fusion | flops 245760 | bytes 1490432 | tf_op jit(solution)/shard_map/jit(_where)/select_n | solution.py:55
  141.8 4.3 %bitcast_select_fusion = f32[30,64,64]{0,1,2:T(8,128)} fusion(f32[30,64,64]{0,1,2:T(8,128)} %rev.8, pred[64,64]{0,1:T(8,128)(4,1)S(1)} %iota_compare_fusion.2), kind=kLoop, calls=%fused_computation.8 | loop fusion | flops 122880 | bytes 987136 | tf_op jit(solution)/shard_map/jit(_where)/select_n | solution.py:57
  146.1 4.0 %copy.104 = f32[30,64,64]{2,1,0:T(8,128)} copy(f32[30,64,64]{0,1,2:T(8,128)} %bitcast_select_fusion) | data formatting | bytes 983040 | tf_op jit(solution)/shard_map/jit(_where)/select_n | solution.py:57
  150.1 3.1 %abs_reduce_fusion = (f32[30,128]{1,0:T(8,128)S(1)}, f32[30,128,128]{2,1,0:T(8,128)}) fusion(f32[128,128]{1,0:T(8,128)S(1)} %fusion.14, f32[30,64,64]{2,1,0:T(8,128)} %copy.104, f32[30,64,64]{2,1,0:T(8,128)S(1)} %copy.103, f32[30,64,64]{2,1,0:T(8,128)S(1)} %copy-done.2, f32[30,64,64]{2,1,0:T(8,128)S(1)} %copy.101), kind=kLoop, calls=%fused_computation.14 | loop fusion | flops 3436800 | bytes 4013056 | tf_op jit(solution)/shard_map/reduce_sum | solution.py:17
  153.5 73.2 %while.12 = (s32[]{:T(128)}, f32[30,128,128]{1,2,0:T(8,128)S(1)}, f32[30,128,128]{2,1,0:T(8,128)}, s32[]{:T(128)}) while((s32[]{:T(128)}, f32[30,128,128]{1,2,0:T(8,128)S(1)}, f32[30,128,128]{2,1,0:T(8,128)}, s32[]{:T(128)}) %tuple.42), condition=%wide.region_6.7_spmd.clone, body=%wide.region_5.6_spmd.clone.sunk | while | flops 1510473728 | bytes 23724112 | solution.py:26
  155.1 4.2 %fusion.42 = f32[30,128,128]{2,1,0:T(8,128)S(1)} fusion(f32[30,128,128]{2,1,0:T(8,128)S(1)} %copy-done, f32[30,128,128]{1,2,0:T(8,128)S(1)} %copy.146), kind=kOutput, calls=%fused_computation.40.clone.1 | convolution fusion | flops 754974720 | bytes 5898240 | tf_op jit(solution)/shard_map/while/body/eval_jaxpr/bij,bjk->bik/dot_general | solution.py:21
  159.3 3.4 %fusion.44 = f32[30,128,128]{1,2,0:T(8,128)S(1)} fusion(f32[30,128,128]{1,2,0:T(8,128)S(1)} %copy.146, f32[30,128,128]{2,1,0:T(8,128)S(1)} %fusion.42, f32[128,128]{1,0:T(8,128)S(1)} %fusion.43), kind=kOutput, calls=%fused_computation.4.clone.1 | convolution fusion | flops 755466240 | bytes 5963776 | tf_op jit(solution)/shard_map/while/body/eval_jaxpr/bij,bjk->bik/dot_general | solution.py:22
  164.2 4.2 %fusion.42 = f32[30,128,128]{2,1,0:T(8,128)S(1)} fusion(f32[30,128,128]{2,1,0:T(8,128)S(1)} %copy-done, f32[30,128,128]{1,2,0:T(8,128)S(1)} %copy.146), kind=kOutput, calls=%fused_computation.40.clone.1 | convolution fusion | flops 754974720 | bytes 5898240 | tf_op jit(solution)/shard_map/while/body/eval_jaxpr/bij,bjk->bik/dot_general | solution.py:21
  168.5 3.4 %fusion.44 = f32[30,128,128]{1,2,0:T(8,128)S(1)} fusion(f32[30,128,128]{1,2,0:T(8,128)S(1)} %copy.146, f32[30,128,128]{2,1,0:T(8,128)S(1)} %fusion.42, f32[128,128]{1,0:T(8,128)S(1)} %fusion.43), kind=kOutput, calls=%fused_computation.4.clone.1 | convolution fusion | flops 755466240 | bytes 5963776 | tf_op jit(solution)/shard_map/while/body/eval_jaxpr/bij,bjk->bik/dot_general | solution.py:22
  173.4 4.2 %fusion.42 = f32[30,128,128]{2,1,0:T(8,128)S(1)} fusion(f32[30,128,128]{2,1,0:T(8,128)S(1)} %copy-done, f32[30,128,128]{1,2,0:T(8,128)S(1)} %copy.146), kind=kOutput, calls=%fused_computation.40.clone.1 | convolution fusion | flops 754974720 | bytes 5898240 | tf_op jit(solution)/shard_map/while/body/eval_jaxpr/bij,bjk->bik/dot_general | solution.py:21
  177.6 3.4 %fusion.44 = f32[30,128,128]{1,2,0:T(8,128)S(1)} fusion(f32[30,128,128]{1,2,0:T(8,128)S(1)} %copy.146, f32[30,128,128]{2,1,0:T(8,128)S(1)} %fusion.42, f32[128,128]{1,0:T(8,128)S(1)} %fusion.43), kind=kOutput, calls=%fused_computation.4.clone.1 | convolution fusion | flops 755466240 | bytes 5963776 | tf_op jit(solution)/shard_map/while/body/eval_jaxpr/bij,bjk->bik/dot_general | solution.py:22
  182.5 4.2 %fusion.42 = f32[30,128,128]{2,1,0:T(8,128)S(1)} fusion(f32[30,128,128]{2,1,0:T(8,128)S(1)} %copy-done, f32[30,128,128]{1,2,0:T(8,128)S(1)} %copy.146), kind=kOutput, calls=%fused_computation.40.clone.1 | convolution fusion | flops 754974720 | bytes 5898240 | tf_op jit(solution)/shard_map/while/body/eval_jaxpr/bij,bjk->bik/dot_general | solution.py:21
  186.8 3.4 %fusion.44 = f32[30,128,128]{1,2,0:T(8,128)S(1)} fusion(f32[30,128,128]{1,2,0:T(8,128)S(1)} %copy.146, f32[30,128,128]{2,1,0:T(8,128)S(1)} %fusion.42, f32[128,128]{1,0:T(8,128)S(1)} %fusion.43), kind=kOutput, calls=%fused_computation.4.clone.1 | convolution fusion | flops 755466240 | bytes 5963776 | tf_op jit(solution)/shard_map/while/body/eval_jaxpr/bij,bjk->bik/dot_general | solution.py:22
  191.7 4.2 %fusion.42 = f32[30,128,128]{2,1,0:T(8,128)S(1)} fusion(f32[30,128,128]{2,1,0:T(8,128)S(1)} %copy-done, f32[30,128,128]{1,2,0:T(8,128)S(1)} %copy.146), kind=kOutput, calls=%fused_computation.40.clone.1 | convolution fusion | flops 754974720 | bytes 5898240 | tf_op jit(solution)/shard_map/while/body/eval_jaxpr/bij,bjk->bik/dot_general | solution.py:21
  195.9 3.4 %fusion.44 = f32[30,128,128]{1,2,0:T(8,128)S(1)} fusion(f32[30,128,128]{1,2,0:T(8,128)S(1)} %copy.146, f32[30,128,128]{2,1,0:T(8,128)S(1)} %fusion.42, f32[128,128]{1,0:T(8,128)S(1)} %fusion.43), kind=kOutput, calls=%fused_computation.4.clone.1 | convolution fusion | flops 755466240 | bytes 5963776 | tf_op jit(solution)/shard_map/while/body/eval_jaxpr/bij,bjk->bik/dot_general | solution.py:22
  200.8 4.2 %fusion.42 = f32[30,128,128]{2,1,0:T(8,128)S(1)} fusion(f32[30,128,128]{2,1,0:T(8,128)S(1)} %copy-done, f32[30,128,128]{1,2,0:T(8,128)S(1)} %copy.146), kind=kOutput, calls=%fused_computation.40.clone.1 | convolution fusion | flops 754974720 | bytes 5898240 | tf_op jit(solution)/shard_map/while/body/eval_jaxpr/bij,bjk->bik/dot_general | solution.py:21
  205.1 3.4 %fusion.44 = f32[30,128,128]{1,2,0:T(8,128)S(1)} fusion(f32[30,128,128]{1,2,0:T(8,128)S(1)} %copy.146, f32[30,128,128]{2,1,0:T(8,128)S(1)} %fusion.42, f32[128,128]{1,0:T(8,128)S(1)} %fusion.43), kind=kOutput, calls=%fused_computation.4.clone.1 | convolution fusion | flops 755466240 | bytes 5963776 | tf_op jit(solution)/shard_map/while/body/eval_jaxpr/bij,bjk->bik/dot_general | solution.py:22
  210.0 4.2 %fusion.42 = f32[30,128,128]{2,1,0:T(8,128)S(1)} fusion(f32[30,128,128]{2,1,0:T(8,128)S(1)} %copy-done, f32[30,128,128]{1,2,0:T(8,128)S(1)} %copy.146), kind=kOutput, calls=%fused_computation.40.clone.1 | convolution fusion | flops 754974720 | bytes 5898240 | tf_op jit(solution)/shard_map/while/body/eval_jaxpr/bij,bjk->bik/dot_general | solution.py:21
  214.2 3.4 %fusion.44 = f32[30,128,128]{1,2,0:T(8,128)S(1)} fusion(f32[30,128,128]{1,2,0:T(8,128)S(1)} %copy.146, f32[30,128,128]{2,1,0:T(8,128)S(1)} %fusion.42, f32[128,128]{1,0:T(8,128)S(1)} %fusion.43), kind=kOutput, calls=%fused_computation.4.clone.1 | convolution fusion | flops 755466240 | bytes 5963776 | tf_op jit(solution)/shard_map/while/body/eval_jaxpr/bij,bjk->bik/dot_general | solution.py:22
  219.2 4.2 %fusion.42 = f32[30,128,128]{2,1,0:T(8,128)S(1)} fusion(f32[30,128,128]{2,1,0:T(8,128)S(1)} %copy-done, f32[30,128,128]{1,2,0:T(8,128)S(1)} %copy.146), kind=kOutput, calls=%fused_computation.40.clone.1 | convolution fusion | flops 754974720 | bytes 5898240 | tf_op jit(solution)/shard_map/while/body/eval_jaxpr/bij,bjk->bik/dot_general | solution.py:21
  223.4 3.4 %fusion.44 = f32[30,128,128]{1,2,0:T(8,128)S(1)} fusion(f32[30,128,128]{1,2,0:T(8,128)S(1)} %copy.146, f32[30,128,128]{2,1,0:T(8,128)S(1)} %fusion.42, f32[128,128]{1,0:T(8,128)S(1)} %fusion.43), kind=kOutput, calls=%fused_computation.4.clone.1 | convolution fusion | flops 755466240 | bytes 5963776 | tf_op jit(solution)/shard_map/while/body/eval_jaxpr/bij,bjk->bik/dot_general | solution.py:22
  238.5 7.0 %all-to-all-start.2 = ((bf16[128,2,200]{2,1,0:T(2,128)(2,1)}), bf16[128,2,200]{2,1,0:T(2,128)(2,1)S(1)}, u32[]{:S(2)}, u32[]{:S(2)}) async-start(bf16[128,2,200]{2,1,0:T(2,128)(2,1)} %reshape.121), calls=%async_computation.2 | async-start | bytes 262144 | tf_op jit(solution)/shard_map/all_to_all | solution.py:110
  248.2 9.6 %all-to-all-done.2 = bf16[128,2,200]{2,1,0:T(2,128)(2,1)S(1)} async-done(((bf16[128,2,200]{2,1,0:T(2,128)(2,1)}), bf16[128,2,200]{2,1,0:T(2,128)(2,1)S(1)}, u32[]{:S(2)}, u32[]{:S(2)}) %all-to-all-start.2) | async-done | bytes 102432 | tf_op jit(solution)/shard_map/all_to_all | solution.py:110
  264.7 8.6 %all-to-all-start.3 = ((bf16[128,2,200]{2,1,0:T(2,128)(2,1)}), bf16[128,2,200]{2,1,0:T(2,128)(2,1)S(1)}, u32[]{:S(2)}, u32[]{:S(2)}) async-start(bf16[128,2,200]{2,1,0:T(2,128)(2,1)} %reshape.123), calls=%async_computation.3 | async-start | bytes 262144 | tf_op jit(solution)/shard_map/all_to_all | solution.py:117
  274.3 11.3 %all-to-all-done.3 = bf16[128,2,200]{2,1,0:T(2,128)(2,1)S(1)} async-done(((bf16[128,2,200]{2,1,0:T(2,128)(2,1)}), bf16[128,2,200]{2,1,0:T(2,128)(2,1)S(1)}, u32[]{:S(2)}, u32[]{:S(2)}) %all-to-all-start.3) | async-done | bytes 102432 | tf_op jit(solution)/shard_map/all_to_all | solution.py:117
  (111 shorter events, 66.1 us)
Async XLA Ops:
  32.4 2.8 copy-start.4
  85.7 37.5 %all-to-all-start.1 = ((f32[128,16,128]{2,1,0:T(8,128)}), f32[128,16,128]{2,1,0:T(8,128)S(1)}, u32[]{:S(2)}, u32[]{:S(2)}) async-start(f32[128,16,128]{2,1,0:T(8,128)} %broadcast_in_dim.50), calls=%async_computation.1 | async-start | bytes 2097152 | tf_op jit(solution)/shard_map/all_to_all | solution.py:68
  92.7 167.2 %all-gather.2.cloned.1.call-start = ((), (), s32[]{:S(2)}) async-start(), calls=%async_computation.4 | async-start | bytes 1638400 | tf_op jit(solution)/shard_map/all_gather | solution.py:103
  123.2 6.9 %copy-start.1 = (f32[128,16,128]{2,1,0:T(8,128)}, f32[128,16,128]{2,1,0:T(8,128)S(1)}, u32[]{:S(2)}) copy-start(f32[128,16,128]{2,1,0:T(8,128)S(1)} %all-to-all-done.1) | copy-start | bytes 3145732
  128.0 2.3 copy-start.3
  146.1 4.0 %copy-start.2 = (f32[30,64,64]{2,1,0:T(8,128)S(1)}, f32[30,64,64]{2,1,0:T(8,128)}, u32[]{:S(2)}) copy-start(f32[30,64,64]{2,1,0:T(8,128)} %get-tuple-element.74) | copy-start | bytes 1474564
  153.5 1.5 copy-start
  162.7 1.5 copy-start
  171.8 1.5 copy-start
  181.0 1.5 copy-start
  190.1 1.5 copy-start
  199.3 1.5 copy-start
  208.5 1.5 copy-start
  217.6 1.5 copy-start
  226.9 3.1 %copy-start.8 = (s32[1,30]{1,0:T(1,128)S(1)}, s32[1,30]{1,0:T(1,128)}, u32[]{:S(2)}) copy-start(s32[1,30]{1,0:T(1,128)} %param.15) | copy-start | bytes 364
  226.9 5.0 %copy-start.6 = (bf16[2,20,1280]{2,0,1:T(2,128)(2,1)S(1)}, bf16[2,20,1280]{2,0,1:T(2,128)(2,1)}, u32[]{:S(2)}) copy-start(bf16[2,20,1280]{2,0,1:T(2,128)(2,1)} %param.12) | copy-start | bytes 307204
  236.3 11.3 %copy-start.7 = (s32[392]{0:T(512)S(1)}, s32[392]{0:T(512)}, u32[]{:S(2)}) copy-start(s32[392]{0:T(512)} %param.14) | copy-start | bytes 4708
  238.5 19.3 %all-to-all-start.2 = ((bf16[128,2,200]{2,1,0:T(2,128)(2,1)}), bf16[128,2,200]{2,1,0:T(2,128)(2,1)S(1)}, u32[]{:S(2)}, u32[]{:S(2)}) async-start(bf16[128,2,200]{2,1,0:T(2,128)(2,1)} %reshape.121), calls=%async_computation.2 | async-start | bytes 262144 | tf_op jit(solution)/shard_map/all_to_all | solution.py:110
  262.0 11.3 %copy-start.5 = (bf16[392,640]{1,0:T(8,128)(2,1)S(1)}, bf16[392,640]{1,0:T(8,128)(2,1)}, u32[]{:S(2)}) copy-start(bf16[392,640]{1,0:T(8,128)(2,1)} %param.13) | copy-start | bytes 1505284
  264.7 20.9 %all-to-all-start.3 = ((bf16[128,2,200]{2,1,0:T(2,128)(2,1)}), bf16[128,2,200]{2,1,0:T(2,128)(2,1)S(1)}, u32[]{:S(2)}, u32[]{:S(2)}) async-start(bf16[128,2,200]{2,1,0:T(2,128)(2,1)} %reshape.123), calls=%async_computation.3 | async-start | bytes 262144 | tf_op jit(solution)/shard_map/all_to_all | solution.py:117
Sparse Core Ops, SparseCore 0:
  230.1 23.0 all-gather.1

commit v3 on v2

--- a/solution.py
+++ b/solution.py
@@ -18,9 +18,9 @@
     approx = identity[None] / norm_scale[:, None, None]
 
     def sweep(sweep_idx, approx):
-        product = jnp.einsum("bij,bjk->bik", damped, approx, precision=lax.Precision.HIGHEST)
+        product = jnp.einsum("bij,bjk->bik", damped, approx, precision=lax.Precision.HIGH)
         return jnp.einsum(
-            "bij,bjk->bik", approx, 2.0 * identity[None] - product, precision=lax.Precision.HIGHEST
+            "bij,bjk->bik", approx, 2.0 * identity[None] - product, precision=lax.Precision.HIGH
         )
 
     return lax.fori_loop(0, NS_ITERS, sweep, approx)
@@ -31,7 +31,7 @@
     rows = lax.broadcasted_iota(jnp.int32, (half, half), 0)
     cols = lax.broadcasted_iota(jnp.int32, (half, half), 1)
     upper_left = blocks[:, :half, :half]
-    lower_right = jnp.flip(blocks[:, half:, half:], (1, 2))
+    lower_right = jnp.swapaxes(blocks[:, half:, half:], 1, 2)
     folded = jnp.where(rows < cols, upper_left, lower_right)
     panel = jnp.concatenate([folded, blocks[:, :half, half:]], axis=2)
     diag = jnp.diagonal(upper_left, axis1=1, axis2=2).reshape(-1, BLK)
@@ -53,8 +53,7 @@
     upper_right = panel[:, :, half:]
     folded_t = jnp.swapaxes(folded, 1, 2)
     upper_left = jnp.where(rows < cols, folded, jnp.where(rows > cols, folded_t, diag[:, :, None]))
-    turned = jnp.flip(folded, (1, 2))
-    lower_right = jnp.where(rows <= cols, turned, jnp.swapaxes(turned, 1, 2))
+    lower_right = jnp.where(rows <= cols, folded_t, folded)
     top = jnp.concatenate([upper_left, upper_right], axis=2)
     bottom = jnp.concatenate([jnp.swapaxes(upper_right, 1, 2), lower_right], axis=2)
     return jnp.concatenate([top, bottom], axis=1), count_total

time: 299 us -> 261 us (0.87)
  matrix products: 64.7 us -> 36.1 us
  local copies, waits for them, and re-layouts: 68.5 us -> 61.3 us
    dot_general x8, matrix products: 33.8 us -> 17.7 us  [sweep(): jnp.einsum('bij,bjk->bik', damped, approx, precision=lax.Precision.HIGH)]
    dot_general x8, matrix products: 26.9 us -> 14.4 us  [sweep(): jnp.einsum('bij,bjk->bik', approx, 2.0 * identity[None] - product, precis...]
    rev x2 -> x0, local copies, waits for them, and re-layouts: 7.59 us -> none  [the longest x1 3.8 us: unpack_symmetric(): turned = jnp.flip(folded, (1, 2))]
    select_n x1 -> x0, other arithmetic: 4.33 us -> none  [unpack_symmetric(): lower_right = jnp.where(rows <= cols, turned, jnp.swapaxes(turned, 1, 2))]
  transfers between devices with their start and end apart: 4 -> 4, of which waited for: 3 -> 3; matrix products, arithmetic and copies ran while one was open for 4% -> 5% of each run, Pallas kernels for 0% -> 0%
where the time goes in v3:
time: 261 us; the launch traced here: 260 us
  local copies, waits for them, and re-layouts  61.3 us (23%)
  waiting for transfers between devices  51.1 us (20%)
  blocking collectives  48.7 us (19%)
  matrix products  36.1 us (14%)
  starting transfers between devices  22.8 us (9%)
  other arithmetic  22.2 us (9%)
  between operations  17.6 us (7%)
    all_to_all x1, blocking collectives, sum_over_fsdp(): lax.all_to_all(packed.reshape(fsdp_size, chunk, BLK), 'fsdp', 0, 0, tiled...  48.7 us
    all_to_all x1, waiting for transfers between devices, sum_over_fsdp(): lax.all_to_all(spread, 'fsdp', 0, 0, tiled=True).reshape(packed.shape)  30.1 us
    unnamed x26, local copies, waits for them, and re-layouts  18.1 us
    dot_general x8, matrix products, sweep(): jnp.einsum('bij,bjk->bik', damped, approx, precision=lax.Precision.HIGH)  17.7 us
    dot_general x8, matrix products, sweep(): jnp.einsum('bij,bjk->bik', approx, 2.0 * identity[None] - product, precis...  14.4 us
    while x24, local copies, waits for them, and re-layouts  12.1 us
    all_to_all x1, waiting for transfers between devices, on_device(): lax.all_to_all(left_done, 'fsdp', split_axis=1, concat_axis=2, tiled=True)  11.3 us
    all_to_all x1, waiting for transfers between devices, on_device(): lax.all_to_all(right_done, 'fsdp', split_axis=2, concat_axis=1, tiled=True)  9.7 us
  transfers between devices with their start and end apart: 4, of which 3 were waited for; matrix products, arithmetic and copies ran while one was open for 5% of the time, Pallas kernels for 0%

profile of v3, /device:TPU:1, one launch (start us, length us, event | category | flops | bytes accessed | tf_op | source)
XLA Modules:
  0.0 260.1 jit_solution(4709799144055043591)
XLA Ops:
  12.6 2.9 %copy.89 = bf16[2,384,1280]{1,2,0:T(8,128)(2,1)S(1)} copy(bf16[2,384,1280]{2,1,0:T(8,128)(2,1)} %param.10) | data formatting | bytes 3932160 | tf_op args[0]
  16.5 1.9 fusion.17
  18.4 4.1 %copy.129 = f32[30,64,64]{0,1,2:T(8,128)} copy(f32[30,64,64]{2,1,0:T(8,128)} %get-tuple-element.73) | data formatting | bytes 983040
  22.5 2.0 copy.128
  26.0 3.6 %bitcast_select_fusion.2 = f32[30,64,64]{0,2,1:T(8,128)} fusion(f32[30,64,64]{0,2,1:T(8,128)} %copy.128, f32[30,64,64]{0,1,2:T(8,128)} %copy.129, pred[64,64]{1,0:T(8,128)(4,1)S(1)} %iota_compare_fusion.4), kind=kLoop, calls=%fused_computation.11 | loop fusion | flops 122880 | bytes 1478656 | tf_op jit(solution)/shard_map/jit(_where)/select_n | solution.py:35
  29.6 2.6 %copy.95 = f32[30,64,64]{2,1,0:T(8,128)S(1)} copy(f32[30,64,64]{0,2,1:T(8,128)} %bitcast_select_fusion.2) | data formatting | bytes 983040 | tf_op jit(solution)/shard_map/jit(_where)/select_n | solution.py:35
  33.0 48.7 %all_to_all.43 = f32[128,16,128]{2,1,0:T(8,128)S(1)} all-to-all(f32[128,16,128]{2,1,0:T(8,128)S(1)} %bitcast.73), channel_id=1, replica_groups=mesh['fsdp'=128,'tensor'=4] {'fsdp'}, dimensions={0} | all-to-all | bytes 2097152 | tf_op jit(solution)/shard_map/all_to_all | solution.py:64
  82.9 7.0 %all-to-all-start.1 = ((f32[128,16,128]{2,1,0:T(8,128)}), f32[128,16,128]{2,1,0:T(8,128)S(1)}, u32[]{:S(2)}, u32[]{:S(2)}) async-start(f32[128,16,128]{2,1,0:T(8,128)} %broadcast_in_dim.50), calls=%async_computation.1 | async-start | bytes 2097152 | tf_op jit(solution)/shard_map/all_to_all | solution.py:67
  90.2 30.1 %all-to-all-done.1 = f32[128,16,128]{2,1,0:T(8,128)S(1)} async-done(((f32[128,16,128]{2,1,0:T(8,128)}), f32[128,16,128]{2,1,0:T(8,128)S(1)}, u32[]{:S(2)}, u32[]{:S(2)}) %all-to-all-start.1) | async-done | bytes 1048608 | tf_op jit(solution)/shard_map/all_to_all | solution.py:67
  122.2 3.0 %copy.98 = f32[30,64,64]{0,1,2:T(8,128)} copy(f32[30,64,64]{2,1,0:T(8,128)S(1)} %get-tuple-element.78) | data formatting | bytes 983040 | tf_op jit(solution)/shard_map/slice | solution.py:52
  125.2 2.1 copy.130
  127.8 7.4 %fusion.9 = (f32[30,64,64]{0,2,1:T(8,128)}, f32[30,64,64]{0,2,1:T(8,128)}) fusion(f32[30,64,64]{0,2,1:T(8,128)} %copy.130, f32[30,64,64]{0,1,2:T(8,128)} %copy.98, f32[30,64]{0,1:T(8,128)S(1)} %copy.99, pred[64,64]{1,0:T(8,128)(4,1)S(1)} %get-tuple-element.80, pred[64,64]{1,0:T(8,128)(4,1)S(1)} %iota_compare_fusion.4, pred[64,64]{1,0:T(8,128)(4,1)S(1)} %get-tuple-element.79), kind=kLoop, calls=%fused_computation.10 | loop fusion | flops 368640 | bytes 1986048 | tf_op jit(solution)/shard_map/jit(_where)/select_n | solution.py:55
  135.2 2.6 copy.100
  137.8 3.5 %copy.102 = f32[30,64,64]{2,1,0:T(8,128)} copy(f32[30,64,64]{0,2,1:T(8,128)} %get-tuple-element.72) | data formatting | bytes 983040 | tf_op jit(solution)/shard_map/jit(_where)/select_n | solution.py:56
  141.3 3.1 %abs_reduce_fusion = (f32[30,128]{1,0:T(8,128)S(1)}, f32[30,128,128]{2,1,0:T(8,128)}) fusion(f32[128,128]{1,0:T(8,128)S(1)} %fusion.14, f32[30,64,64]{2,1,0:T(8,128)} %copy.102, f32[30,64,64]{2,1,0:T(8,128)S(1)} %copy.101, f32[30,64,64]{2,1,0:T(8,128)S(1)} %copy-done.2, f32[30,64,64]{2,1,0:T(8,128)S(1)} %copy.100), kind=kLoop, calls=%fused_computation.15 | loop fusion | flops 3436800 | bytes 4013056 | tf_op jit(solution)/shard_map/reduce_sum | solution.py:17
  144.7 44.7 %while.12 = (s32[]{:T(128)}, f32[30,128,128]{1,2,0:T(8,128)S(1)}, f32[30,128,128]{2,1,0:T(8,128)}, s32[]{:T(128)}) while((s32[]{:T(128)}, f32[30,128,128]{1,2,0:T(8,128)S(1)}, f32[30,128,128]{2,1,0:T(8,128)}, s32[]{:T(128)}) %tuple.43), condition=%wide.region_6.7_spmd.clone, body=%wide.region_5.6_spmd.clone.sunk | while | flops 755499008 | bytes 23724112 | solution.py:26
  146.3 2.2 fusion.42
  151.8 2.2 fusion.42
  157.4 2.2 fusion.42
  163.0 2.2 fusion.42
  168.6 2.2 fusion.42
  174.2 2.2 fusion.42
  179.8 2.2 fusion.42
  185.3 2.2 fusion.42
  197.1 1.8 copy.114
  201.1 7.1 %all-to-all-start.2 = ((bf16[128,2,200]{2,1,0:T(2,128)(2,1)}), bf16[128,2,200]{2,1,0:T(2,128)(2,1)S(1)}, u32[]{:S(2)}, u32[]{:S(2)}) async-start(bf16[128,2,200]{2,1,0:T(2,128)(2,1)} %reshape.121), calls=%async_computation.2 | async-start | bytes 262144 | tf_op jit(solution)/shard_map/all_to_all | solution.py:109
  208.3 2.1 select_bitcast_fusion
  211.0 9.7 %all-to-all-done.2 = bf16[128,2,200]{2,1,0:T(2,128)(2,1)S(1)} async-done(((bf16[128,2,200]{2,1,0:T(2,128)(2,1)}), bf16[128,2,200]{2,1,0:T(2,128)(2,1)S(1)}, u32[]{:S(2)}, u32[]{:S(2)}) %all-to-all-start.2) | async-done | bytes 102432 | tf_op jit(solution)/shard_map/all_to_all | solution.py:109
  222.8 2.1 convolution_convert_fusion
  227.6 8.4 %all-to-all-start.3 = ((bf16[128,2,200]{2,1,0:T(2,128)(2,1)}), bf16[128,2,200]{2,1,0:T(2,128)(2,1)S(1)}, u32[]{:S(2)}, u32[]{:S(2)}) async-start(bf16[128,2,200]{2,1,0:T(2,128)(2,1)} %reshape.123), calls=%async_computation.3 | async-start | bytes 262144 | tf_op jit(solution)/shard_map/all_to_all | solution.py:116
  236.9 11.3 %all-to-all-done.3 = bf16[128,2,200]{2,1,0:T(2,128)(2,1)S(1)} async-done(((bf16[128,2,200]{2,1,0:T(2,128)(2,1)}), bf16[128,2,200]{2,1,0:T(2,128)(2,1)S(1)}, u32[]{:S(2)}, u32[]{:S(2)}) %all-to-all-start.3) | async-done | bytes 102432 | tf_op jit(solution)/shard_map/all_to_all | solution.py:116
  249.2 2.3 copy.123
  (108 shorter events, 55.2 us)
Async XLA Ops:
  29.6 2.8 %copy-start.4 = (f32[30,64,64]{2,1,0:T(8,128)S(1)}, f32[30,64,64]{2,1,0:T(8,128)}, u32[]{:S(2)}) copy-start(f32[30,64,64]{2,1,0:T(8,128)} %get-tuple-element.74) | copy-start | bytes 1474564
  82.9 37.5 %all-to-all-start.1 = ((f32[128,16,128]{2,1,0:T(8,128)}), f32[128,16,128]{2,1,0:T(8,128)S(1)}, u32[]{:S(2)}, u32[]{:S(2)}) async-start(f32[128,16,128]{2,1,0:T(8,128)} %broadcast_in_dim.50), calls=%async_computation.1 | async-start | bytes 2097152 | tf_op jit(solution)/shard_map/all_to_all | solution.py:67
  89.9 132.9 %all-gather.2.cloned.1.call-start = ((), (), s32[]{:S(2)}) async-start(), calls=%async_computation.4 | async-start | bytes 1638400 | tf_op jit(solution)/shard_map/all_gather | solution.py:102
  120.4 6.9 %copy-start.1 = (f32[128,16,128]{2,1,0:T(8,128)}, f32[128,16,128]{2,1,0:T(8,128)S(1)}, u32[]{:S(2)}) copy-start(f32[128,16,128]{2,1,0:T(8,128)S(1)} %all-to-all-done.1) | copy-start | bytes 3145732
  125.2 2.3 copy-start.3
  137.8 3.5 %copy-start.2 = (f32[30,64,64]{2,1,0:T(8,128)S(1)}, f32[30,64,64]{2,1,0:T(8,128)}, u32[]{:S(2)}) copy-start(f32[30,64,64]{2,1,0:T(8,128)} %get-tuple-element.76) | copy-start | bytes 1474564
  144.7 1.5 copy-start
  150.3 1.5 copy-start
  155.9 1.5 copy-start
  161.5 1.5 copy-start
  167.0 1.5 copy-start
  172.6 1.5 copy-start
  178.2 1.5 copy-start
  183.8 1.5 copy-start
  189.5 3.1 %copy-start.8 = (s32[1,30]{1,0:T(1,128)S(1)}, s32[1,30]{1,0:T(1,128)}, u32[]{:S(2)}) copy-start(s32[1,30]{1,0:T(1,128)} %param.15) | copy-start | bytes 364
  189.5 5.0 %copy-start.6 = (bf16[2,20,1280]{2,0,1:T(2,128)(2,1)S(1)}, bf16[2,20,1280]{2,0,1:T(2,128)(2,1)}, u32[]{:S(2)}) copy-start(bf16[2,20,1280]{2,0,1:T(2,128)(2,1)} %param.12) | copy-start | bytes 307204
  198.9 11.4 %copy-start.7 = (s32[392]{0:T(512)S(1)}, s32[392]{0:T(512)}, u32[]{:S(2)}) copy-start(s32[392]{0:T(512)} %param.14) | copy-start | bytes 4708
  201.1 19.6 %all-to-all-start.2 = ((bf16[128,2,200]{2,1,0:T(2,128)(2,1)}), bf16[128,2,200]{2,1,0:T(2,128)(2,1)S(1)}, u32[]{:S(2)}, u32[]{:S(2)}) async-start(bf16[128,2,200]{2,1,0:T(2,128)(2,1)} %reshape.121), calls=%async_computation.2 | async-start | bytes 262144 | tf_op jit(solution)/shard_map/all_to_all | solution.py:109
  224.9 11.1 %copy-start.5 = (bf16[392,640]{1,0:T(8,128)(2,1)S(1)}, bf16[392,640]{1,0:T(8,128)(2,1)}, u32[]{:S(2)}) copy-start(bf16[392,640]{1,0:T(8,128)(2,1)} %param.13) | copy-start | bytes 1505284
  227.6 20.7 %all-to-all-start.3 = ((bf16[128,2,200]{2,1,0:T(2,128)(2,1)}), bf16[128,2,200]{2,1,0:T(2,128)(2,1)S(1)}, u32[]{:S(2)}, u32[]{:S(2)}) async-start(bf16[128,2,200]{2,1,0:T(2,128)(2,1)} %reshape.123), calls=%async_computation.3 | async-start | bytes 262144 | tf_op jit(solution)/shard_map/all_to_all | solution.py:116
Sparse Core Ops, SparseCore 0:
  192.7 23.0 all-gather.1

commit v4 on v3

--- a/solution.py
+++ b/solution.py
@@ -28,13 +28,11 @@
 
 def pack_symmetric(blocks, count_part, fsdp_size):
     half = BLK // 2
-    rows = lax.broadcasted_iota(jnp.int32, (half, half), 0)
-    cols = lax.broadcasted_iota(jnp.int32, (half, half), 1)
-    upper_left = blocks[:, :half, :half]
-    lower_right = jnp.swapaxes(blocks[:, half:, half:], 1, 2)
-    folded = jnp.where(rows < cols, upper_left, lower_right)
-    panel = jnp.concatenate([folded, blocks[:, :half, half:]], axis=2)
-    diag = jnp.diagonal(upper_left, axis1=1, axis2=2).reshape(-1, BLK)
+    rows = lax.broadcasted_iota(jnp.int32, (half, BLK), 0)
+    lanes = lax.broadcasted_iota(jnp.int32, (half, BLK), 1)
+    bottom = blocks[:, half:, :]
+    panel = jnp.where(lanes >= rows, blocks[:, :half, :], jnp.roll(bottom, half, axis=2))
+    diag = jnp.sum(jnp.where(lanes == rows + half, bottom, 0.0), axis=2).reshape(-1, BLK)
     count_row = jnp.zeros((1, BLK), jnp.float32).at[0, 0].set(count_part)
     body = jnp.concatenate([panel.reshape(-1, BLK), diag, count_row], axis=0)
     total = -(-body.shape[0] // fsdp_size) * fsdp_size
@@ -47,16 +45,15 @@
     diag_rows = block_total * half // BLK
     diag = summed[block_total * half : block_total * half + diag_rows].reshape(block_total, half)
     count_total = summed[block_total * half + diag_rows, 0]
-    rows = lax.broadcasted_iota(jnp.int32, (half, half), 0)
-    cols = lax.broadcasted_iota(jnp.int32, (half, half), 1)
-    folded = panel[:, :, :half]
-    upper_right = panel[:, :, half:]
-    folded_t = jnp.swapaxes(folded, 1, 2)
-    upper_left = jnp.where(rows < cols, folded, jnp.where(rows > cols, folded_t, diag[:, :, None]))
-    lower_right = jnp.where(rows <= cols, folded_t, folded)
-    top = jnp.concatenate([upper_left, upper_right], axis=2)
-    bottom = jnp.concatenate([jnp.swapaxes(upper_right, 1, 2), lower_right], axis=2)
-    return jnp.concatenate([top, bottom], axis=1), count_total
+    rows = lax.broadcasted_iota(jnp.int32, (half, BLK), 0)
+    lanes = lax.broadcasted_iota(jnp.int32, (half, BLK), 1)
+    top = jnp.where(lanes >= rows, panel, 0.0)
+    turned = jnp.roll(panel, half, axis=2)
+    bottom = jnp.where((lanes >= half) & (lanes - half < rows), turned, 0.0)
+    bottom = jnp.where(lanes - half == rows, diag[:, :, None], bottom)
+    tri = jnp.concatenate([top, bottom], axis=1)
+    eye = lax.broadcasted_iota(jnp.int32, (BLK, BLK), 0) == lax.broadcasted_iota(jnp.int32, (BLK, BLK), 1)
+    return jnp.where(eye, tri, tri + jnp.swapaxes(tri, 1, 2)), count_total
 
 
 def sum_over_fsdp(packed, fsdp_size):

time: 261 us -> 231 us (0.89)
  local copies, waits for them, and re-layouts: 61.3 us -> 40 us
  other arithmetic: 22.2 us -> 13.9 us
    select_n x2, other arithmetic: 11 us -> 0.69 us  [the longest x1 0.59 us: unpack_symmetric(): bottom = jnp.where(lanes - half == rows, diag[:, :, None], bottom)]
    select_n x3 -> x0, local copies, waits for them, and re-layouts: 8.67 us -> none  [the longest x1 3.47 us: unpack_symmetric(): lower_right = jnp.where(rows <= cols, folded_t, folded)]
    unnamed x26 -> x17, local copies, waits for them, and re-layouts: 18.1 us -> 10.6 us
    slice x3 -> x2, local copies, waits for them, and re-layouts: 6.64 us -> 0.69 us  [the longest x1 0.35 us: pack_symmetric(): jnp.roll(bottom, half, axis=2)]
    concatenate x0 -> x1, local copies, waits for them, and re-layouts: none -> 2.83 us  [unpack_symmetric(): tri = jnp.concatenate([top, bottom], axis=1)]
where the time goes in v4:
time: 231 us
  waiting for transfers between devices  51 us (22%)
  blocking collectives  48.7 us (21%)
  local copies, waits for them, and re-layouts  40 us (17%)
  matrix products  36.1 us (16%)
  starting transfers between devices  22.8 us (10%)
  between operations  17.6 us (8%)
  other arithmetic  13.9 us (6%)
    all_to_all x1, blocking collectives, sum_over_fsdp(): lax.all_to_all(packed.reshape(fsdp_size, chunk, BLK), 'fsdp', 0, 0, tiled...  48.7 us
    all_to_all x1, waiting for transfers between devices, sum_over_fsdp(): lax.all_to_all(spread, 'fsdp', 0, 0, tiled=True).reshape(packed.shape)  30.1 us
    dot_general x8, matrix products, sweep(): jnp.einsum('bij,bjk->bik', damped, approx, precision=lax.Precision.HIGH)  17.7 us
    dot_general x8, matrix products, sweep(): jnp.einsum('bij,bjk->bik', approx, 2.0 * identity[None] - product, precis...  14.4 us
    while x24, local copies, waits for them, and re-layouts  12.1 us
    all_to_all x1, waiting for transfers between devices, on_device(): lax.all_to_all(left_done, 'fsdp', split_axis=1, concat_axis=2, tiled=True)  11.3 us
    unnamed x17, local copies, waits for them, and re-layouts  10.6 us
    all_to_all x1, waiting for transfers between devices, on_device(): lax.all_to_all(right_done, 'fsdp', split_axis=2, concat_axis=1, tiled=True)  9.62 us
  transfers between devices with their start and end apart: 4, of which 3 were waited for; matrix products, arithmetic and copies ran while one was open for 5% of the time, Pallas kernels for 0%

profile of v4, /device:TPU:1, one launch (start us, length us, event | category | flops | bytes accessed | tf_op | source)
XLA Modules:
  0.0 230.5 jit_solution(15274977157308426659)
XLA Ops:
  12.6 2.9 %copy.88 = bf16[2,384,1280]{1,2,0:T(8,128)(2,1)S(1)} copy(bf16[2,384,1280]{2,1,0:T(8,128)(2,1)} %param.10) | data formatting | bytes 3932160 | tf_op args[0]
  17.9 48.7 %all_to_all.43 = f32[128,16,128]{2,1,0:T(8,128)S(1)} all-to-all(f32[128,16,128]{2,1,0:T(8,128)S(1)} %bitcast.68), channel_id=1, replica_groups=mesh['fsdp'=128,'tensor'=4] {'fsdp'}, dimensions={0} | all-to-all | bytes 2097152 | tf_op jit(solution)/shard_map/all_to_all | solution.py:61
  67.7 7.0 %all-to-all-start.1 = ((f32[128,16,128]{2,1,0:T(8,128)}), f32[128,16,128]{2,1,0:T(8,128)S(1)}, u32[]{:S(2)}, u32[]{:S(2)}) async-start(f32[128,16,128]{2,1,0:T(8,128)} %broadcast_in_dim.63), calls=%async_computation.1 | async-start | bytes 2097152 | tf_op jit(solution)/shard_map/all_to_all | solution.py:64
  75.1 30.1 %all-to-all-done.1 = f32[128,16,128]{2,1,0:T(8,128)S(1)} async-done(((f32[128,16,128]{2,1,0:T(8,128)}), f32[128,16,128]{2,1,0:T(8,128)S(1)}, u32[]{:S(2)}, u32[]{:S(2)}) %all-to-all-start.1) | async-done | bytes 1048608 | tf_op jit(solution)/shard_map/all_to_all | solution.py:64
  108.6 2.8 %copy.92 = f32[30,128,128]{1,2,0:T(8,128)} copy(f32[30,128,128]{2,1,0:T(8,128)} %pad_maximum_fusion.1) | data formatting | bytes 3932160 | tf_op jit(solution)/shard_map/concatenate | solution.py:54
  111.5 3.3 %abs_reduce_fusion = (f32[30,128]{1,0:T(8,128)S(1)}, f32[30,128,128]{2,1,0:T(8,128)}) fusion(f32[128,128]{1,0:T(8,128)S(1)} %fusion.16, f32[30,128,128]{1,2,0:T(8,128)} %copy.92, f32[30,64,128]{2,1,0:T(8,128)S(1)} %fusion.13, f32[30,64,128]{2,1,0:T(8,128)S(1)} %broadcast_select_fusion, pred[128,128]{1,0:T(8,128)(4,1)S(1)} %iota_compare_fusion.1), kind=kLoop, calls=%fused_computation.12 | loop fusion | flops 3436800 | bytes 5995520 | tf_op jit(solution)/shard_map/reduce_sum | solution.py:17
  115.1 44.7 %while.12 = (s32[]{:T(128)}, f32[30,128,128]{1,2,0:T(8,128)S(1)}, f32[30,128,128]{2,1,0:T(8,128)}, s32[]{:T(128)}) while((s32[]{:T(128)}, f32[30,128,128]{1,2,0:T(8,128)S(1)}, f32[30,128,128]{2,1,0:T(8,128)}, s32[]{:T(128)}) %tuple.41), condition=%wide.region_7.8_spmd.clone, body=%wide.region_6.7_spmd.clone.sunk | while | flops 755499008 | bytes 23724112 | solution.py:26
  116.7 2.2 fusion.45
  118.9 1.8 fusion.47
  122.2 2.2 fusion.45
  124.5 1.8 fusion.47
  127.8 2.2 fusion.45
  130.0 1.8 fusion.47
  133.4 2.2 fusion.45
  135.6 1.8 fusion.47
  139.0 2.2 fusion.45
  141.2 1.8 fusion.47
  144.6 2.2 fusion.45
  146.8 1.8 fusion.47
  150.2 2.2 fusion.45
  152.4 1.8 fusion.47
  155.7 2.2 fusion.45
  158.0 1.8 fusion.47
  161.3 1.7 slice.73
  167.5 1.8 copy.103
  171.5 7.0 %all-to-all-start.2 = ((bf16[128,2,200]{2,1,0:T(2,128)(2,1)}), bf16[128,2,200]{2,1,0:T(2,128)(2,1)S(1)}, u32[]{:S(2)}, u32[]{:S(2)}) async-start(bf16[128,2,200]{2,1,0:T(2,128)(2,1)} %reshape.115), calls=%async_computation.2 | async-start | bytes 262144 | tf_op jit(solution)/shard_map/all_to_all | solution.py:106
  178.5 2.1 select_bitcast_fusion
  181.2 9.6 %all-to-all-done.2 = bf16[128,2,200]{2,1,0:T(2,128)(2,1)S(1)} async-done(((bf16[128,2,200]{2,1,0:T(2,128)(2,1)}), bf16[128,2,200]{2,1,0:T(2,128)(2,1)S(1)}, u32[]{:S(2)}, u32[]{:S(2)}) %all-to-all-start.2) | async-done | bytes 102432 | tf_op jit(solution)/shard_map/all_to_all | solution.py:106
  193.0 2.1 convolution_convert_fusion
  197.7 8.6 %all-to-all-start.3 = ((bf16[128,2,200]{2,1,0:T(2,128)(2,1)}), bf16[128,2,200]{2,1,0:T(2,128)(2,1)S(1)}, u32[]{:S(2)}, u32[]{:S(2)}) async-start(bf16[128,2,200]{2,1,0:T(2,128)(2,1)} %reshape.117), calls=%async_computation.3 | async-start | bytes 262144 | tf_op jit(solution)/shard_map/all_to_all | solution.py:113
  207.3 11.3 %all-to-all-done.3 = bf16[128,2,200]{2,1,0:T(2,128)(2,1)S(1)} async-done(((bf16[128,2,200]{2,1,0:T(2,128)(2,1)}), bf16[128,2,200]{2,1,0:T(2,128)(2,1)S(1)}, u32[]{:S(2)}, u32[]{:S(2)}) %all-to-all-start.3) | async-done | bytes 102432 | tf_op jit(solution)/shard_map/all_to_all | solution.py:113
  219.6 2.3 %copy.112 = bf16[2,128,20,10]{2,1,0,3:T(8,128)(2,1)S(1)} copy(bf16[2,128,20,10]{3,0,2,1:T(2,128)(2,1)S(1)} %bitcast.67) | data formatting | bytes 204800 | tf_op jit(solution)/shard_map/all_to_all | solution.py:113
  (96 shorter events, 39.2 us)
Async XLA Ops:
  67.7 37.5 %all-to-all-start.1 = ((f32[128,16,128]{2,1,0:T(8,128)}), f32[128,16,128]{2,1,0:T(8,128)S(1)}, u32[]{:S(2)}, u32[]{:S(2)}) async-start(f32[128,16,128]{2,1,0:T(8,128)} %broadcast_in_dim.63), calls=%async_computation.1 | async-start | bytes 2097152 | tf_op jit(solution)/shard_map/all_to_all | solution.py:64
  74.7 118.2 %all-gather.2.cloned.1.call-start = ((), (), s32[]{:S(2)}) async-start(), calls=%async_computation.4 | async-start | bytes 1638400 | tf_op jit(solution)/shard_map/all_gather | solution.py:99
  105.2 1.0 copy-start.1
  115.1 1.5 copy-start
  120.7 1.5 copy-start
  126.3 1.5 copy-start
  131.9 1.5 copy-start
  137.4 1.5 copy-start
  143.0 1.5 copy-start
  148.6 1.5 copy-start
  154.2 1.5 copy-start
  159.9 3.1 %copy-start.5 = (s32[1,30]{1,0:T(1,128)S(1)}, s32[1,30]{1,0:T(1,128)}, u32[]{:S(2)}) copy-start(s32[1,30]{1,0:T(1,128)} %param.15) | copy-start | bytes 364
  159.9 5.0 %copy-start.3 = (bf16[2,20,1280]{2,0,1:T(2,128)(2,1)S(1)}, bf16[2,20,1280]{2,0,1:T(2,128)(2,1)}, u32[]{:S(2)}) copy-start(bf16[2,20,1280]{2,0,1:T(2,128)(2,1)} %param.12) | copy-start | bytes 307204
  169.4 11.3 %copy-start.4 = (s32[392]{0:T(512)S(1)}, s32[392]{0:T(512)}, u32[]{:S(2)}) copy-start(s32[392]{0:T(512)} %param.14) | copy-start | bytes 4708
  171.5 19.3 %all-to-all-start.2 = ((bf16[128,2,200]{2,1,0:T(2,128)(2,1)}), bf16[128,2,200]{2,1,0:T(2,128)(2,1)S(1)}, u32[]{:S(2)}, u32[]{:S(2)}) async-start(bf16[128,2,200]{2,1,0:T(2,128)(2,1)} %reshape.115), calls=%async_computation.2 | async-start | bytes 262144 | tf_op jit(solution)/shard_map/all_to_all | solution.py:106
  195.0 11.3 %copy-start.2 = (bf16[392,640]{1,0:T(8,128)(2,1)S(1)}, bf16[392,640]{1,0:T(8,128)(2,1)}, u32[]{:S(2)}) copy-start(bf16[392,640]{1,0:T(8,128)(2,1)} %param.13) | copy-start | bytes 1505284
  197.7 20.9 %all-to-all-start.3 = ((bf16[128,2,200]{2,1,0:T(2,128)(2,1)}), bf16[128,2,200]{2,1,0:T(2,128)(2,1)S(1)}, u32[]{:S(2)}, u32[]{:S(2)}) async-start(bf16[128,2,200]{2,1,0:T(2,128)(2,1)} %reshape.117), calls=%async_computation.3 | async-start | bytes 262144 | tf_op jit(solution)/shard_map/all_to_all | solution.py:113
Sparse Core Ops, SparseCore 0:
  163.1 23.0 all-gather.1

commit v5 on v4

--- a/solution.py
+++ b/solution.py
@@ -86,7 +86,11 @@
     blocks_sum, count_total = unpack_symmetric(summed, block_total)
     divisor = row_count * fsdp_size
     factors = blocks_sum / divisor
-    inv = newton_inverse(factors)
+    core = lax.axis_index("fsdp") % 2
+    share = block_total // 2
+    mine = newton_inverse(lax.dynamic_slice_in_dim(factors, core * share, share, axis=0))
+    other = lax.ppermute(mine, "fsdp", [(i, i ^ 1) for i in range(fsdp_size)])
+    inv = jnp.where(core == 0, jnp.concatenate([mine, other]), jnp.concatenate([other, mine]))
     own_table = owner_pos[0]
     slot = lax.axis_index("fsdp")
     hit = own_table == slot

time: 231 us -> 207 us (0.90)
  matrix products: 36.1 us -> 20.7 us
  local copies, waits for them, and re-layouts: 40 us -> 24.9 us
  starting transfers between devices: 22.8 us -> 27.1 us
    while x24 -> x8, local copies, waits for them, and re-layouts: 12.1 us -> 0.67 us
    dot_general x8, matrix products: 17.7 us -> 9.18 us  [sweep(): jnp.einsum('bij,bjk->bik', damped, approx, precision=lax.Precision.HIGH)]
    dot_general x8, matrix products: 14.4 us -> 7.73 us  [sweep(): jnp.einsum('bij,bjk->bik', approx, 2.0 * identity[None] - product, precis...]
    ppermute x0 -> x1, starting transfers between devices: none -> 3.92 us  [on_device(): other = lax.ppermute(mine, 'fsdp', [(i, i ^ 1) for i in range(fsdp_size)])]
  transfers between devices with their start and end apart: 4 -> 5, of which waited for: 3 -> 4; matrix products, arithmetic and copies ran while one was open for 5% -> 5% of each run, Pallas kernels for 0% -> 0%
where the time goes in v5:
time: 207 us; the launch traced here: 206 us
  waiting for transfers between devices  53 us (26%)
  blocking collectives  48.7 us (24%)
  starting transfers between devices  27.1 us (13%)
  local copies, waits for them, and re-layouts  24.9 us (12%)
  matrix products  20.7 us (10%)
  between operations  17.6 us (9%)
  other arithmetic  13.6 us (7%)
    all_to_all x1, blocking collectives, sum_over_fsdp(): lax.all_to_all(packed.reshape(fsdp_size, chunk, BLK), 'fsdp', 0, 0, tiled...  48.7 us
    all_to_all x1, waiting for transfers between devices, sum_over_fsdp(): lax.all_to_all(spread, 'fsdp', 0, 0, tiled=True).reshape(packed.shape)  30.2 us
    all_to_all x1, waiting for transfers between devices, on_device(): lax.all_to_all(right_done, 'fsdp', split_axis=2, concat_axis=1, tiled=True)  11.6 us
    unnamed x17, local copies, waits for them, and re-layouts  10.7 us
    all_to_all x1, starting transfers between devices, on_device(): lax.all_to_all(left_done, 'fsdp', split_axis=1, concat_axis=2, tiled=True)  10.6 us
    dot_general x8, matrix products, sweep(): jnp.einsum('bij,bjk->bik', damped, approx, precision=lax.Precision.HIGH)  9.18 us
    all_to_all x1, waiting for transfers between devices, on_device(): lax.all_to_all(left_done, 'fsdp', split_axis=1, concat_axis=2, tiled=True)  9.11 us
    dot_general x8, matrix products, sweep(): jnp.einsum('bij,bjk->bik', approx, 2.0 * identity[None] - product, precis...  7.73 us
  transfers between devices with their start and end apart: 5, of which 4 were waited for; matrix products, arithmetic and copies ran while one was open for 5% of the time, Pallas kernels for 0%

profile of v5, /device:TPU:1, one launch (start us, length us, event | category | flops | bytes accessed | tf_op | source)
XLA Modules:
  0.0 206.0 jit_solution(11027111805147949148)
XLA Ops:
  7.8 1.3 convert_reduce_fusion
  10.5 1.6 copy.94
  12.6 2.8 %copy.92 = bf16[2,384,1280]{1,2,0:T(8,128)(2,1)S(1)} copy(bf16[2,384,1280]{2,1,0:T(8,128)(2,1)} %param.10) | data formatting | bytes 3932160 | tf_op args[0]
  17.9 48.7 %all_to_all.43 = f32[128,16,128]{2,1,0:T(8,128)S(1)} all-to-all(f32[128,16,128]{2,1,0:T(8,128)S(1)} %bitcast.70), channel_id=1, replica_groups=mesh['fsdp'=128,'tensor'=4] {'fsdp'}, dimensions={0} | all-to-all | bytes 2097152 | tf_op jit(solution)/shard_map/all_to_all | solution.py:61
  67.7 7.0 %all-to-all-start.1 = ((f32[128,16,128]{2,1,0:T(8,128)}), f32[128,16,128]{2,1,0:T(8,128)S(1)}, u32[]{:S(2)}, u32[]{:S(2)}) async-start(f32[128,16,128]{2,1,0:T(8,128)} %broadcast_in_dim.63), calls=%async_computation.1 | async-start | bytes 2097152 | tf_op jit(solution)/shard_map/all_to_all | solution.py:64
  75.0 30.2 %all-to-all-done.1 = f32[128,16,128]{2,1,0:T(8,128)S(1)} async-done(((f32[128,16,128]{2,1,0:T(8,128)}), f32[128,16,128]{2,1,0:T(8,128)S(1)}, u32[]{:S(2)}, u32[]{:S(2)}) %all-to-all-start.1) | async-done | bytes 1048608 | tf_op jit(solution)/shard_map/all_to_all | solution.py:64
  107.2 1.4 pad_maximum_fusion
  108.6 2.8 %copy.96 = f32[30,128,128]{1,2,0:T(8,128)} copy(f32[30,128,128]{2,1,0:T(8,128)} %pad_maximum_fusion) | data formatting | bytes 3932160 | tf_op jit(solution)/shard_map/concatenate | solution.py:54
  111.5 1.5 abs_reduce_fusion
  113.3 18.0 %while.12 = (s32[]{:T(128)}, f32[15,128,128]{1,2,0:T(8,128)S(1)}, f32[15,128,128]{2,1,0:T(8,128)S(1)}, s32[]{:T(128)}) while((s32[]{:T(128)}, f32[15,128,128]{1,2,0:T(8,128)S(1)}, f32[15,128,128]{2,1,0:T(8,128)S(1)}, s32[]{:T(128)}) %tuple.42), condition=%wide.region_7.8_spmd.clone, body=%wide.region_6.7_spmd.clone.sunk | while | flops 377765888 | bytes 7995445 | solution.py:26
  113.4 1.1 convolution_subtract_fusion.2
  115.7 1.1 convolution_subtract_fusion.2
  117.9 1.1 convolution_subtract_fusion.2
  120.2 1.1 convolution_subtract_fusion.2
  122.4 1.1 convolution_subtract_fusion.2
  124.7 1.1 convolution_subtract_fusion.2
  126.9 1.1 convolution_subtract_fusion.2
  129.2 1.1 convolution_subtract_fusion.2
  131.6 3.9 %collective-permute-start = (f32[15,128,128]{2,1,0:T(8,128)S(1)}, f32[15,128,128]{2,1,0:T(8,128)S(1)}, u32[]{:S(2)}, u32[]{:S(2)}) collective-permute-start(f32[15,128,128]{2,1,0:T(8,128)S(1)} %copy.98), channel_id=1, source_target_pairs={{0,4},{4,0},{8,12},{12,8},{16,20},{20,16},{24,28},{28,24},{32,36},... | collective-permute-start | bytes 2949128 | tf_op jit(solution)/shard_map/ppermute | solution.py:92
  135.6 2.0 collective-permute-done
  137.5 1.6 fusion.14
  143.3 1.2 slice.74
  145.3 1.2 reshape.117
  146.5 5.5 %all-to-all-start.2 = ((bf16[128,2,200]{2,1,0:T(2,128)(2,1)}), bf16[128,2,200]{2,1,0:T(2,128)(2,1)S(1)}, u32[]{:S(2)}, u32[]{:S(2)}) async-start(bf16[128,2,200]{2,1,0:T(2,128)(2,1)} %reshape.117), calls=%async_computation.2 | async-start | bytes 262144 | tf_op jit(solution)/shard_map/all_to_all | solution.py:110
  152.7 11.6 %all-to-all-done.2 = bf16[128,2,200]{2,1,0:T(2,128)(2,1)S(1)} async-done(((bf16[128,2,200]{2,1,0:T(2,128)(2,1)}), bf16[128,2,200]{2,1,0:T(2,128)(2,1)S(1)}, u32[]{:S(2)}, u32[]{:S(2)}) %all-to-all-start.2) | async-done | bytes 102432 | tf_op jit(solution)/shard_map/all_to_all | solution.py:110
  165.1 1.4 reshape.116
  166.5 2.1 %convolution_convert_fusion = bf16[2,20,128,10]{2,3,1,0:T(8,128)(2,1)S(1)} fusion(bf16[2,20,128,128]{3,2,1,0:T(8,128)(2,1)} %all-gather.2.cloned.1.call-done, bf16[2,20,128,10]{2,1,3,0:T(8,128)(2,1)S(1)} %reshape.116), kind=kOutput, calls=%fused_computation.11 | convolution fusion | flops 13158400 | bytes 1515520 | tf_op jit(solution)/shard_map/lbij,lbjc->lbic/dot_general | solution.py:113
  169.6 1.6 reshape.119
  171.2 10.6 %all-to-all-start.3 = ((bf16[128,2,200]{2,1,0:T(2,128)(2,1)}), bf16[128,2,200]{2,1,0:T(2,128)(2,1)S(1)}, u32[]{:S(2)}, u32[]{:S(2)}) async-start(bf16[128,2,200]{2,1,0:T(2,128)(2,1)} %reshape.119), calls=%async_computation.3 | async-start | bytes 262144 | tf_op jit(solution)/shard_map/all_to_all | solution.py:117
  182.8 2.1 %select_bitcast_fusion = f32[1,1,128,128]{3,2,1,0:T(8,128)} fusion(f32[30,128,128]{2,1,0:T(8,128)} %get-tuple-element.67, s32[]{:T(128)S(6)} %select_n.69, pred[]{:T(512)} %compare_reduce_fusion.1), kind=kLoop, calls=%fused_computation.28 | loop fusion | flops 16384 | bytes 131077 | tf_op jit(solution)/shard_map/broadcast_in_dim | solution.py:99
  184.9 9.1 %all-to-all-done.3 = bf16[128,2,200]{2,1,0:T(2,128)(2,1)S(1)} async-done(((bf16[128,2,200]{2,1,0:T(2,128)(2,1)}), bf16[128,2,200]{2,1,0:T(2,128)(2,1)S(1)}, u32[]{:S(2)}, u32[]{:S(2)}) %all-to-all-start.3) | async-done | bytes 102432 | tf_op jit(solution)/shard_map/all_to_all | solution.py:117
  195.0 2.3 %copy.117 = bf16[2,128,20,10]{2,1,0,3:T(8,128)(2,1)S(1)} copy(bf16[2,128,20,10]{3,0,2,1:T(2,128)(2,1)S(1)} %bitcast.68) | data formatting | bytes 204800 | tf_op jit(solution)/shard_map/all_to_all | solution.py:117
  (81 shorter events, 25.2 us)
Async XLA Ops:
  67.7 37.5 %all-to-all-start.1 = ((f32[128,16,128]{2,1,0:T(8,128)}), f32[128,16,128]{2,1,0:T(8,128)S(1)}, u32[]{:S(2)}, u32[]{:S(2)}) async-start(f32[128,16,128]{2,1,0:T(8,128)} %broadcast_in_dim.63), calls=%async_computation.1 | async-start | bytes 2097152 | tf_op jit(solution)/shard_map/all_to_all | solution.py:64
  74.7 91.7 %all-gather.2.cloned.1.call-start = ((), (), s32[]{:S(2)}) async-start(), calls=%async_computation.4 | async-start | bytes 1638400 | tf_op jit(solution)/shard_map/all_gather | solution.py:103
  105.2 1.0 copy-start
  131.6 5.9 %collective-permute-start = (f32[15,128,128]{2,1,0:T(8,128)S(1)}, f32[15,128,128]{2,1,0:T(8,128)S(1)}, u32[]{:S(2)}, u32[]{:S(2)}) collective-permute-start(f32[15,128,128]{2,1,0:T(8,128)S(1)} %copy.98), channel_id=1, source_target_pairs={{0,4},{4,0},{8,12},{12,8},{16,20},{20,16},{24,28},{28,24},{32,36},... | collective-permute-start | bytes 2949128 | tf_op jit(solution)/shard_map/ppermute | solution.py:92
  135.6 4.4 %copy-start.4 = (s32[1,30]{1,0:T(1,128)S(1)}, s32[1,30]{1,0:T(1,128)}, u32[]{:S(2)}) copy-start(s32[1,30]{1,0:T(1,128)} %param.15) | copy-start | bytes 364
  135.6 6.3 %copy-start.2 = (bf16[2,20,1280]{2,0,1:T(2,128)(2,1)S(1)}, bf16[2,20,1280]{2,0,1:T(2,128)(2,1)}, u32[]{:S(2)}) copy-start(bf16[2,20,1280]{2,0,1:T(2,128)(2,1)} %param.12) | copy-start | bytes 307204
  144.5 7.5 %copy-start.3 = (s32[392]{0:T(512)S(1)}, s32[392]{0:T(512)}, u32[]{:S(2)}) copy-start(s32[392]{0:T(512)} %param.14) | copy-start | bytes 4708
  146.5 17.9 %all-to-all-start.2 = ((bf16[128,2,200]{2,1,0:T(2,128)(2,1)}), bf16[128,2,200]{2,1,0:T(2,128)(2,1)S(1)}, u32[]{:S(2)}, u32[]{:S(2)}) async-start(bf16[128,2,200]{2,1,0:T(2,128)(2,1)} %reshape.117), calls=%async_computation.2 | async-start | bytes 262144 | tf_op jit(solution)/shard_map/all_to_all | solution.py:110
  168.5 13.3 %copy-start.1 = (bf16[392,640]{1,0:T(8,128)(2,1)S(1)}, bf16[392,640]{1,0:T(8,128)(2,1)}, u32[]{:S(2)}) copy-start(bf16[392,640]{1,0:T(8,128)(2,1)} %param.13) | copy-start | bytes 1505284
  171.2 22.8 %all-to-all-start.3 = ((bf16[128,2,200]{2,1,0:T(2,128)(2,1)}), bf16[128,2,200]{2,1,0:T(2,128)(2,1)S(1)}, u32[]{:S(2)}, u32[]{:S(2)}) async-start(bf16[128,2,200]{2,1,0:T(2,128)(2,1)} %reshape.119), calls=%async_computation.3 | async-start | bytes 262144 | tf_op jit(solution)/shard_map/all_to_all | solution.py:117
Sparse Core Ops, SparseCore 0:
  140.1 21.5 all-gather.1

commit v6 on v5

--- a/solution.py
+++ b/solution.py
@@ -1,9 +1,13 @@
 import jax
 import jax.numpy as jnp
 from jax import lax
-from jax.sharding import PartitionSpec as P
+import numpy as np
+from jax.sharding import Mesh, PartitionSpec as P
 
 BLK = 128
+FSDP_SIZE = 128
+CHIP_AXES = ("y", "z")
+FSDP = ("y", "z", "core")
 NS_ITERS = 8
 
 
@@ -57,15 +61,27 @@
 
 
 def sum_over_fsdp(packed, fsdp_size):
-    chunk = packed.shape[0] // fsdp_size
-    pieces = lax.all_to_all(packed.reshape(fsdp_size, chunk, BLK), "fsdp", 0, 0, tiled=True)
+    core = lax.axis_index("core")
+    chips = fsdp_size // 2
+    halves = packed.reshape(2, packed.shape[0] // 2, BLK)
+    send = jnp.where(core == 0, halves[1], halves[0])
+    keep = jnp.where(core == 0, halves[0], halves[1])
+    part = keep + lax.ppermute(send, "core", [(0, 1), (1, 0)])
+    chunk = part.shape[0] // chips
+    pieces = lax.all_to_all(part.reshape(chips, chunk, BLK), CHIP_AXES, 0, 0, tiled=True)
     mine = jnp.sum(pieces, axis=0)
-    spread = jnp.broadcast_to(mine[None], (fsdp_size, chunk, BLK))
-    return lax.all_to_all(spread, "fsdp", 0, 0, tiled=True).reshape(packed.shape)
+    spread = jnp.broadcast_to(mine[None], (chips, chunk, BLK))
+    own_half = lax.all_to_all(spread, CHIP_AXES, 0, 0, tiled=True).reshape(part.shape)
+    other_half = lax.ppermute(own_half, "core", [(0, 1), (1, 0)])
+    return jnp.where(
+        core == 0,
+        jnp.concatenate([own_half, other_half]),
+        jnp.concatenate([other_half, own_half]),
+    )
 
 
 def on_device(layer_inputs, out_grads, weight_grad, emb_grad, counts, owner_pos):
-    fsdp_size = lax.axis_size("fsdp")
+    fsdp_size = FSDP_SIZE
     layers, row_count, inner_local = layer_inputs.shape
     width_local = out_grads.shape[2]
     a_count = inner_local // BLK
@@ -86,13 +102,13 @@
     blocks_sum, count_total = unpack_symmetric(summed, block_total)
     divisor = row_count * fsdp_size
     factors = blocks_sum / divisor
-    core = lax.axis_index("fsdp") % 2
+    core = lax.axis_index(FSDP) % 2
     share = block_total // 2
     mine = newton_inverse(lax.dynamic_slice_in_dim(factors, core * share, share, axis=0))
-    other = lax.ppermute(mine, "fsdp", [(i, i ^ 1) for i in range(fsdp_size)])
+    other = lax.ppermute(mine, FSDP, [(i, i ^ 1) for i in range(fsdp_size)])
     inv = jnp.where(core == 0, jnp.concatenate([mine, other]), jnp.concatenate([other, mine]))
     own_table = owner_pos[0]
-    slot = lax.axis_index("fsdp")
+    slot = lax.axis_index(FSDP)
     hit = own_table == slot
     pick = jnp.argmax(hit)
     held = lax.dynamic_index_in_dim(inv, pick, axis=0, keepdims=True)
@@ -107,14 +123,14 @@
         "ldbi,lbij->ldbj", grad_split, a_low, preferred_element_type=jnp.float32
     )
     right_done = right_done.reshape(layers, d_local, inner_local).astype(jnp.bfloat16)
-    columns = lax.all_to_all(right_done, "fsdp", split_axis=2, concat_axis=1, tiled=True)
+    columns = lax.all_to_all(right_done, FSDP, split_axis=2, concat_axis=1, tiled=True)
     full_width = columns.shape[1]
     column_blocks = columns.reshape(layers, full_width // BLK, BLK, columns.shape[2])
     left_done = jnp.einsum(
         "lbij,lbjc->lbic", g_all, column_blocks, preferred_element_type=jnp.float32
     )
     left_done = left_done.reshape(columns.shape).astype(jnp.bfloat16)
-    update = lax.all_to_all(left_done, "fsdp", split_axis=1, concat_axis=2, tiled=True)
+    update = lax.all_to_all(left_done, FSDP, split_axis=1, concat_axis=2, tiled=True)
     vocab_total = counts.shape[0] * fsdp_size
     frequency = counts.astype(jnp.float32) * vocab_total / count_total
     emb_update = (emb_grad.astype(jnp.float32) / (frequency + EDAMP)[:, None]).astype(jnp.bfloat16)
@@ -122,18 +138,19 @@
 
 
 def solution(mesh):
+    fine = Mesh(np.asarray(mesh.devices).reshape(8, 8, 2, -1), FSDP + ("tensor",))
     placed = (
-        P(None, "fsdp", "tensor"),
-        P(None, "fsdp", "tensor"),
-        P(None, "fsdp", "tensor"),
-        P("fsdp", "tensor"),
-        P("fsdp"),
+        P(None, FSDP, "tensor"),
+        P(None, FSDP, "tensor"),
+        P(None, FSDP, "tensor"),
+        P(FSDP, "tensor"),
+        P(FSDP),
         P("tensor", None),
     )
     return jax.shard_map(
         on_device,
-        mesh=mesh,
+        mesh=fine,
         in_specs=placed,
-        out_specs=(P(None, "fsdp", "tensor"), P("tensor", "fsdp", None, None), P("fsdp", "tensor")),
+        out_specs=(P(None, FSDP, "tensor"), P("tensor", FSDP, None, None), P(FSDP, "tensor")),
         check_vma=False,
     )

time: 207 us -> 191 us (0.923)
  blocking collectives: 48.7 us -> 27.5 us
  starting transfers between devices: 27.1 us -> 41.2 us
  waiting for transfers between devices: 53 us -> 42 us
    all_to_all x1, blocking collectives: 48.7 us -> 27.5 us  [sum_over_fsdp(): lax.all_to_all(part.reshape(chips, chunk, BLK), CHIP_AXES, 0, 0, tiled=True)]
    all_to_all x3, waiting for transfers between devices: 51 us -> 36.9 us  [the longest x1 16.1 us: sum_over_fsdp(): lax.all_to_all(spread, CHIP_AXES, 0, 0, tiled=True).reshape(part.shape)]
    ppermute x1 -> x3, starting transfers between devices: 3.92 us -> 16.7 us  [the longest x1 8.75 us: sum_over_fsdp(): part = keep + lax.ppermute(send, 'core', [(0, 1), (1, 0)])]
    ppermute x1 -> x3, waiting for transfers between devices: 1.96 us -> 5.09 us  [the longest x1 2.14 us: on_device(): other = lax.ppermute(mine, FSDP, [(i, i ^ 1) for i in range(fsdp_size)])]
  transfers between devices with their start and end apart: 5 -> 7, of which waited for: 4 -> 6; matrix products, arithmetic and copies ran while one was open for 5% -> 6% of each run, Pallas kernels for 0% -> 0%
where the time goes in v6:
time: 191 us; the launch traced here: 190 us
  waiting for transfers between devices  42 us (22%)
  starting transfers between devices  41.2 us (22%)
  blocking collectives  27.5 us (14%)
  local copies, waits for them, and re-layouts  25.7 us (13%)
  matrix products  20.7 us (11%)
  between operations  17.7 us (9%)
  other arithmetic  14.9 us (8%)
    all_to_all x1, blocking collectives, sum_over_fsdp(): lax.all_to_all(part.reshape(chips, chunk, BLK), CHIP_AXES, 0, 0, tiled=True)  27.5 us
    all_to_all x1, waiting for transfers between devices, sum_over_fsdp(): lax.all_to_all(spread, CHIP_AXES, 0, 0, tiled=True).reshape(part.shape)  16.1 us
    all_to_all x1, waiting for transfers between devices, on_device(): lax.all_to_all(right_done, FSDP, split_axis=2, concat_axis=1, tiled=True)  11.6 us
    unnamed x17, local copies, waits for them, and re-layouts  10.7 us
    all_to_all x1, starting transfers between devices, on_device(): lax.all_to_all(left_done, FSDP, split_axis=1, concat_axis=2, tiled=True)  10.5 us
    dot_general x8, matrix products, sweep(): jnp.einsum('bij,bjk->bik', damped, approx, precision=lax.Precision.HIGH)  9.18 us
    all_to_all x1, waiting for transfers between devices, on_device(): lax.all_to_all(left_done, FSDP, split_axis=1, concat_axis=2, tiled=True)  9.11 us
    ppermute x1, starting transfers between devices, sum_over_fsdp(): part = keep + lax.ppermute(send, 'core', [(0, 1), (1, 0)])  8.75 us
  transfers between devices with their start and end apart: 7, of which 6 were waited for; matrix products, arithmetic and copies ran while one was open for 6% of the time, Pallas kernels for 0%

profile of v6, /device:TPU:1, one launch (start us, length us, event | category | flops | bytes accessed | tf_op | source)
XLA Modules:
  0.0 190.1 jit_solution(10418899611213481238)
XLA Ops:
  7.8 1.3 convert_reduce_fusion
  10.5 1.6 copy.94
  12.6 2.8 %copy.92 = bf16[2,384,1280]{1,2,0:T(8,128)(2,1)S(1)} copy(bf16[2,384,1280]{2,1,0:T(8,128)(2,1)} %param.10) | data formatting | bytes 3932160 | tf_op args[0]
  18.0 8.8 %collective-permute-start = (f32[1024,128]{1,0:T(8,128)S(1)}, f32[1024,128]{1,0:T(8,128)S(1)}, u32[]{:S(2)}, u32[]{:S(2)}) collective-permute-start(f32[1024,128]{1,0:T(8,128)S(1)} %bitcast_select_fusion), channel_id=1, source_target_pairs={{0,4},{4,0},{1,5},{5,1},{2,6},{6,2},{3,7},{7,3},{8,12},{12,8},{9,1... | collective-permute-start | bytes 1572872 | tf_op jit(solution)/shard_map/ppermute | solution.py:69
  26.7 1.5 collective-permute-done
  28.3 27.5 %all_to_all.43 = f32[64,16,128]{2,1,0:T(8,128)S(1)} all-to-all(f32[64,16,128]{2,1,0:T(8,128)S(1)} %bitcast.80), channel_id=1, replica_groups=mesh['y'=8,'z'=8,'core'=2,'tensor'=4] {'y','z'}, dimensions={0} | all-to-all | bytes 1048576 | tf_op jit(solution)/shard_map/all_to_all | solution.py:71
  56.7 7.6 %all-to-all-start.1 = ((f32[64,16,128]{2,1,0:T(8,128)}), f32[64,16,128]{2,1,0:T(8,128)S(1)}, u32[]{:S(2)}, u32[]{:S(2)}) async-start(f32[64,16,128]{2,1,0:T(8,128)} %broadcast_in_dim.63), calls=%async_computation.1 | async-start | bytes 1048576 | tf_op jit(solution)/shard_map/all_to_all | solution.py:74
  64.6 16.1 %all-to-all-done.1 = f32[64,16,128]{2,1,0:T(8,128)S(1)} async-done(((f32[64,16,128]{2,1,0:T(8,128)}), f32[64,16,128]{2,1,0:T(8,128)S(1)}, u32[]{:S(2)}, u32[]{:S(2)}) %all-to-all-start.1) | async-done | bytes 524320 | tf_op jit(solution)/shard_map/all_to_all | solution.py:74
  80.7 5.6 %collective-permute-start.1 = (f32[1024,128]{1,0:T(8,128)S(1)}, f32[1024,128]{1,0:T(8,128)S(1)}, u32[]{:S(2)}, u32[]{:S(2)}) collective-permute-start(f32[1024,128]{1,0:T(8,128)S(1)} %bitcast.78), channel_id=1, source_target_pairs={{0,4},{4,0},{1,5},{5,1},{2,6},{6,2},{3,7},{7,3},{8,12},{12,8},{9,1... | collective-permute-start | bytes 1572872 | tf_op jit(solution)/shard_map/ppermute | solution.py:75
  86.5 1.4 collective-permute-done.1
  89.0 1.3 fusion.18
  90.4 1.8 fusion.8
  92.1 1.4 pad_maximum_fusion
  93.6 2.8 %copy.96 = f32[30,128,128]{1,2,0:T(8,128)} copy(f32[30,128,128]{2,1,0:T(8,128)} %pad_maximum_fusion) | data formatting | bytes 3932160 | tf_op jit(solution)/shard_map/concatenate | solution.py:58
  96.4 1.5 abs_reduce_fusion
  98.2 18.0 %while.12 = (s32[]{:T(128)}, f32[15,128,128]{1,2,0:T(8,128)S(1)}, f32[15,128,128]{2,1,0:T(8,128)S(1)}, s32[]{:T(128)}) while((s32[]{:T(128)}, f32[15,128,128]{1,2,0:T(8,128)S(1)}, f32[15,128,128]{2,1,0:T(8,128)S(1)}, s32[]{:T(128)}) %tuple.42), condition=%wide.region_7.8_spmd.clone, body=%wide.region_6.7_spmd.clone.sunk | while | flops 377765888 | bytes 7995445 | solution.py:30
  111.8 1.1 convolution_subtract_fusion.2
  114.1 1.1 convolution_subtract_fusion.2
  116.5 2.3 %collective-permute-start.2 = (f32[15,128,128]{2,1,0:T(8,128)S(1)}, f32[15,128,128]{2,1,0:T(8,128)S(1)}, u32[]{:S(2)}, u32[]{:S(2)}) collective-permute-start(f32[15,128,128]{2,1,0:T(8,128)S(1)} %copy.98), channel_id=1, source_target_pairs={{0,4},{4,0},{8,12},{12,8},{16,20},{20,16},{24,28},{28,24},{32,36},... | collective-permute-start | bytes 2949128 | tf_op jit(solution)/shard_map/ppermute | solution.py:108
  118.9 2.1 %collective-permute-done.2 = f32[15,128,128]{2,1,0:T(8,128)S(1)} collective-permute-done((f32[15,128,128]{2,1,0:T(8,128)S(1)}, f32[15,128,128]{2,1,0:T(8,128)S(1)}, u32[]{:S(2)}, u32[]{:S(2)}) %collective-permute-start.2) | collective-permute-done | bytes 983072 | tf_op jit(solution)/shard_map/ppermute | solution.py:108
  121.0 1.6 fusion.15
  126.7 1.2 slice.92
  128.8 1.2 reshape.121
  129.9 6.4 %all-to-all-start.2 = ((bf16[128,2,200]{2,1,0:T(2,128)(2,1)}), bf16[128,2,200]{2,1,0:T(2,128)(2,1)S(1)}, u32[]{:S(2)}, u32[]{:S(2)}) async-start(bf16[128,2,200]{2,1,0:T(2,128)(2,1)} %reshape.121), calls=%async_computation.2 | async-start | bytes 262144 | tf_op jit(solution)/shard_map/all_to_all | solution.py:126
  137.0 11.6 %all-to-all-done.2 = bf16[128,2,200]{2,1,0:T(2,128)(2,1)S(1)} async-done(((bf16[128,2,200]{2,1,0:T(2,128)(2,1)}), bf16[128,2,200]{2,1,0:T(2,128)(2,1)S(1)}, u32[]{:S(2)}, u32[]{:S(2)}) %all-to-all-start.2) | async-done | bytes 102432 | tf_op jit(solution)/shard_map/all_to_all | solution.py:126
  149.3 1.4 reshape.120
  150.7 2.1 %convolution_convert_fusion = bf16[2,20,128,10]{2,3,1,0:T(8,128)(2,1)S(1)} fusion(bf16[2,20,128,128]{3,2,1,0:T(8,128)(2,1)} %all-gather.2.cloned.1.call-done, bf16[2,20,128,10]{2,1,3,0:T(8,128)(2,1)S(1)} %reshape.120), kind=kOutput, calls=%fused_computation.11 | convolution fusion | flops 13158400 | bytes 1515520 | tf_op jit(solution)/shard_map/lbij,lbjc->lbic/dot_general | solution.py:129
  153.9 1.6 reshape.123
  155.5 10.5 %all-to-all-start.3 = ((bf16[128,2,200]{2,1,0:T(2,128)(2,1)}), bf16[128,2,200]{2,1,0:T(2,128)(2,1)S(1)}, u32[]{:S(2)}, u32[]{:S(2)}) async-start(bf16[128,2,200]{2,1,0:T(2,128)(2,1)} %reshape.123), calls=%async_computation.3 | async-start | bytes 262144 | tf_op jit(solution)/shard_map/all_to_all | solution.py:133
  166.9 2.1 %select_bitcast_fusion = f32[1,1,128,128]{3,2,1,0:T(8,128)} fusion(f32[30,128,128]{2,1,0:T(8,128)} %get-tuple-element.67, s32[]{:T(128)S(6)} %select_n.94, pred[]{:T(512)} %compare_reduce_fusion.1), kind=kLoop, calls=%fused_computation.32 | loop fusion | flops 16384 | bytes 131077 | tf_op jit(solution)/shard_map/broadcast_in_dim | solution.py:115
  169.1 9.1 %all-to-all-done.3 = bf16[128,2,200]{2,1,0:T(2,128)(2,1)S(1)} async-done(((bf16[128,2,200]{2,1,0:T(2,128)(2,1)}), bf16[128,2,200]{2,1,0:T(2,128)(2,1)S(1)}, u32[]{:S(2)}, u32[]{:S(2)}) %all-to-all-start.3) | async-done | bytes 102432 | tf_op jit(solution)/shard_map/all_to_all | solution.py:133
  179.2 2.3 %copy.117 = bf16[2,128,20,10]{2,1,0,3:T(8,128)(2,1)S(1)} copy(bf16[2,128,20,10]{3,0,2,1:T(2,128)(2,1)S(1)} %bitcast.72) | data formatting | bytes 204800 | tf_op jit(solution)/shard_map/all_to_all | solution.py:133
  (89 shorter events, 31.1 us)
Async XLA Ops:
  18.0 10.3 %collective-permute-start = (f32[1024,128]{1,0:T(8,128)S(1)}, f32[1024,128]{1,0:T(8,128)S(1)}, u32[]{:S(2)}, u32[]{:S(2)}) collective-permute-start(f32[1024,128]{1,0:T(8,128)S(1)} %bitcast_select_fusion), channel_id=1, source_target_pairs={{0,4},{4,0},{1,5},{5,1},{2,6},{6,2},{3,7},{7,3},{8,12},{12,8},{9,1... | collective-permute-start | bytes 1572872 | tf_op jit(solution)/shard_map/ppermute | solution.py:69
  56.7 24.0 %all-to-all-start.1 = ((f32[64,16,128]{2,1,0:T(8,128)}), f32[64,16,128]{2,1,0:T(8,128)S(1)}, u32[]{:S(2)}, u32[]{:S(2)}) async-start(f32[64,16,128]{2,1,0:T(8,128)} %broadcast_in_dim.63), calls=%async_computation.1 | async-start | bytes 1048576 | tf_op jit(solution)/shard_map/all_to_all | solution.py:74
  64.4 86.4 %all-gather.2.cloned.1.call-start = ((), (), s32[]{:S(2)}) async-start(), calls=%async_computation.4 | async-start | bytes 1638400 | tf_op jit(solution)/shard_map/all_gather | solution.py:119
  80.7 7.2 %collective-permute-start.1 = (f32[1024,128]{1,0:T(8,128)S(1)}, f32[1024,128]{1,0:T(8,128)S(1)}, u32[]{:S(2)}, u32[]{:S(2)}) collective-permute-start(f32[1024,128]{1,0:T(8,128)S(1)} %bitcast.78), channel_id=1, source_target_pairs={{0,4},{4,0},{1,5},{5,1},{2,6},{6,2},{3,7},{7,3},{8,12},{12,8},{9,1... | collective-permute-start | bytes 1572872 | tf_op jit(solution)/shard_map/ppermute | solution.py:75
  88.0 1.0 copy-start
  116.5 4.5 %collective-permute-start.2 = (f32[15,128,128]{2,1,0:T(8,128)S(1)}, f32[15,128,128]{2,1,0:T(8,128)S(1)}, u32[]{:S(2)}, u32[]{:S(2)}) collective-permute-start(f32[15,128,128]{2,1,0:T(8,128)S(1)} %copy.98), channel_id=1, source_target_pairs={{0,4},{4,0},{8,12},{12,8},{16,20},{20,16},{24,28},{28,24},{32,36},... | collective-permute-start | bytes 2949128 | tf_op jit(solution)/shard_map/ppermute | solution.py:108
  118.8 4.6 %copy-start.4 = (s32[1,30]{1,0:T(1,128)S(1)}, s32[1,30]{1,0:T(1,128)}, u32[]{:S(2)}) copy-start(s32[1,30]{1,0:T(1,128)} %param.15) | copy-start | bytes 364
  118.9 6.5 %copy-start.2 = (bf16[2,20,1280]{2,0,1:T(2,128)(2,1)S(1)}, bf16[2,20,1280]{2,0,1:T(2,128)(2,1)}, u32[]{:S(2)}) copy-start(bf16[2,20,1280]{2,0,1:T(2,128)(2,1)} %param.12) | copy-start | bytes 307204
  127.9 8.4 %copy-start.3 = (s32[392]{0:T(512)S(1)}, s32[392]{0:T(512)}, u32[]{:S(2)}) copy-start(s32[392]{0:T(512)} %param.14) | copy-start | bytes 4708
  129.9 18.7 %all-to-all-start.2 = ((bf16[128,2,200]{2,1,0:T(2,128)(2,1)}), bf16[128,2,200]{2,1,0:T(2,128)(2,1)S(1)}, u32[]{:S(2)}, u32[]{:S(2)}) async-start(bf16[128,2,200]{2,1,0:T(2,128)(2,1)} %reshape.121), calls=%async_computation.2 | async-start | bytes 262144 | tf_op jit(solution)/shard_map/all_to_all | solution.py:126
  152.8 13.2 %copy-start.1 = (bf16[392,640]{1,0:T(8,128)(2,1)S(1)}, bf16[392,640]{1,0:T(8,128)(2,1)}, u32[]{:S(2)}) copy-start(bf16[392,640]{1,0:T(8,128)(2,1)} %param.13) | copy-start | bytes 1505284
  155.5 22.7 %all-to-all-start.3 = ((bf16[128,2,200]{2,1,0:T(2,128)(2,1)}), bf16[128,2,200]{2,1,0:T(2,128)(2,1)S(1)}, u32[]{:S(2)}, u32[]{:S(2)}) async-start(bf16[128,2,200]{2,1,0:T(2,128)(2,1)} %reshape.123), calls=%async_computation.3 | async-start | bytes 262144 | tf_op jit(solution)/shard_map/all_to_all | solution.py:133
Sparse Core Ops, SparseCore 0:
  123.5 22.2 all-gather.1

commit v7 on v6

--- a/solution.py
+++ b/solution.py
@@ -123,14 +123,24 @@
         "ldbi,lbij->ldbj", grad_split, a_low, preferred_element_type=jnp.float32
     )
     right_done = right_done.reshape(layers, d_local, inner_local).astype(jnp.bfloat16)
-    columns = lax.all_to_all(right_done, FSDP, split_axis=2, concat_axis=1, tiled=True)
+    chips = fsdp_size // 2
+    by_chip = lax.all_to_all(right_done, CHIP_AXES, split_axis=2, concat_axis=1, tiled=True)
+    by_core = lax.all_to_all(by_chip, "core", split_axis=2, concat_axis=1, tiled=True)
+    col_count = by_core.shape[2]
+    columns = jnp.swapaxes(by_core.reshape(layers, 2, chips, d_local, col_count), 1, 2).reshape(
+        layers, fsdp_size * d_local, col_count
+    )
     full_width = columns.shape[1]
     column_blocks = columns.reshape(layers, full_width // BLK, BLK, columns.shape[2])
     left_done = jnp.einsum(
         "lbij,lbjc->lbic", g_all, column_blocks, preferred_element_type=jnp.float32
     )
     left_done = left_done.reshape(columns.shape).astype(jnp.bfloat16)
-    update = lax.all_to_all(left_done, FSDP, split_axis=1, concat_axis=2, tiled=True)
+    back = jnp.swapaxes(left_done.reshape(layers, chips, 2, d_local, col_count), 1, 2).reshape(
+        layers, fsdp_size * d_local, col_count
+    )
+    back = lax.all_to_all(back, "core", split_axis=1, concat_axis=2, tiled=True)
+    update = lax.all_to_all(back, CHIP_AXES, split_axis=1, concat_axis=2, tiled=True)
     vocab_total = counts.shape[0] * fsdp_size
     frequency = counts.astype(jnp.float32) * vocab_total / count_total
     emb_update = (emb_grad.astype(jnp.float32) / (frequency + EDAMP)[:, None]).astype(jnp.bfloat16)

time: 191 us -> 205 us (1.073)
  local copies, waits for them, and re-layouts: 25.7 us -> 38.3 us
  blocking collectives: 27.5 us -> 36.9 us
  starting transfers between devices: 41.2 us -> 34.2 us
    all_to_all x0 -> x2, blocking collectives: none -> 9.4 us  [the longest x1 5.53 us: on_device(): lax.all_to_all(by_chip, 'core', split_axis=2, concat_axis=1, tiled=True)]
    all_to_all x2, starting transfers between devices: 16.8 us -> 9.83 us  [the longest x1 5.22 us: on_device(): lax.all_to_all(right_done, CHIP_AXES, split_axis=2, concat_axis=1, tiled=...]
    unnamed x17 -> x18, local copies, waits for them, and re-layouts: 10.7 us -> 14.8 us
    reshape x1 -> x2, local copies, waits for them, and re-layouts: 1.35 us -> 5.24 us  [the longest x1 3.61 us: on_device(): jnp.swapaxes(left_done.reshape(layers, chips, 2, d_local, col_count), 1, 2)]
    all_to_all x3 -> x7, local copies, waits for them, and re-layouts: 3.12 us -> 5.06 us  [the longest x2 2.08 us: on_device(): lax.all_to_all(back, CHIP_AXES, split_axis=1, concat_axis=2, tiled=True)]
where the time goes in v7:
time: 205 us; the launch traced here: 204 us
  waiting for transfers between devices  40.7 us (20%)
  local copies, waits for them, and re-layouts  38.3 us (19%)
  blocking collectives  36.9 us (18%)
  starting transfers between devices  34.2 us (17%)
  matrix products  20.7 us (10%)
  between operations  17.8 us (9%)
  other arithmetic  14.9 us (7%)
    all_to_all x1, blocking collectives, sum_over_fsdp(): lax.all_to_all(part.reshape(chips, chunk, BLK), CHIP_AXES, 0, 0, tiled=True)  27.5 us
    all_to_all x1, waiting for transfers between devices, sum_over_fsdp(): lax.all_to_all(spread, CHIP_AXES, 0, 0, tiled=True).reshape(part.shape)  16.1 us
    unnamed x18, local copies, waits for them, and re-layouts  14.8 us
    all_to_all x1, waiting for transfers between devices, on_device(): lax.all_to_all(right_done, CHIP_AXES, split_axis=2, concat_axis=1, tiled=...  10.8 us
    dot_general x8, matrix products, sweep(): jnp.einsum('bij,bjk->bik', damped, approx, precision=lax.Precision.HIGH)  9.18 us
    ppermute x1, starting transfers between devices, sum_over_fsdp(): part = keep + lax.ppermute(send, 'core', [(0, 1), (1, 0)])  8.75 us
    all_to_all x1, waiting for transfers between devices, on_device(): lax.all_to_all(back, CHIP_AXES, split_axis=1, concat_axis=2, tiled=True)  8.63 us
    dot_general x8, matrix products, sweep(): jnp.einsum('bij,bjk->bik', approx, 2.0 * identity[None] - product, precis...  7.73 us
  transfers between devices with their start and end apart: 7, of which 6 were waited for; matrix products, arithmetic and copies ran while one was open for 6% of the time, Pallas kernels for 0%

profile of v7, /device:TPU:1, one launch (start us, length us, event | category | flops | bytes accessed | tf_op | source)
XLA Modules:
  0.0 203.9 jit_solution(2348593961993137250)
XLA Ops:
  10.5 1.6 copy.126
  12.6 2.8 %copy.124 = bf16[2,384,1280]{1,2,0:T(8,128)(2,1)S(1)} copy(bf16[2,384,1280]{2,1,0:T(8,128)(2,1)} %param.10) | data formatting | bytes 3932160 | tf_op args[0]
  18.0 8.8 %collective-permute-start = (f32[1024,128]{1,0:T(8,128)S(1)}, f32[1024,128]{1,0:T(8,128)S(1)}, u32[]{:S(2)}, u32[]{:S(2)}) collective-permute-start(f32[1024,128]{1,0:T(8,128)S(1)} %bitcast_select_fusion), channel_id=1, source_target_pairs={{0,4},{4,0},{1,5},{5,1},{2,6},{6,2},{3,7},{7,3},{8,12},{12,8},{9,1... | collective-permute-start | bytes 1572872 | tf_op jit(solution)/shard_map/ppermute | solution.py:69
  26.7 1.5 collective-permute-done
  28.3 27.5 %all_to_all.79 = f32[64,16,128]{2,1,0:T(8,128)S(1)} all-to-all(f32[64,16,128]{2,1,0:T(8,128)S(1)} %bitcast.109), channel_id=1, replica_groups=mesh['y'=8,'z'=8,'core'=2,'tensor'=4] {'y','z'}, dimensions={0} | all-to-all | bytes 1048576 | tf_op jit(solution)/shard_map/all_to_all | solution.py:71
  56.7 7.6 %all-to-all-start.1 = ((f32[64,16,128]{2,1,0:T(8,128)}), f32[64,16,128]{2,1,0:T(8,128)S(1)}, u32[]{:S(2)}, u32[]{:S(2)}) async-start(f32[64,16,128]{2,1,0:T(8,128)} %broadcast_in_dim.63), calls=%async_computation.1 | async-start | bytes 1048576 | tf_op jit(solution)/shard_map/all_to_all | solution.py:74
  64.6 16.1 %all-to-all-done.1 = f32[64,16,128]{2,1,0:T(8,128)S(1)} async-done(((f32[64,16,128]{2,1,0:T(8,128)}), f32[64,16,128]{2,1,0:T(8,128)S(1)}, u32[]{:S(2)}, u32[]{:S(2)}) %all-to-all-start.1) | async-done | bytes 524320 | tf_op jit(solution)/shard_map/all_to_all | solution.py:74
  80.7 5.6 %collective-permute-start.1 = (f32[1024,128]{1,0:T(8,128)S(1)}, f32[1024,128]{1,0:T(8,128)S(1)}, u32[]{:S(2)}, u32[]{:S(2)}) collective-permute-start(f32[1024,128]{1,0:T(8,128)S(1)} %bitcast.107), channel_id=1, source_target_pairs={{0,4},{4,0},{1,5},{5,1},{2,6},{6,2},{3,7},{7,3},{8,12},{12,8},{9,1... | collective-permute-start | bytes 1572872 | tf_op jit(solution)/shard_map/ppermute | solution.py:75
  86.5 1.4 collective-permute-done.1
  90.4 1.8 fusion.8
  92.1 1.4 pad_maximum_fusion
  93.6 2.8 %copy.128 = f32[30,128,128]{1,2,0:T(8,128)} copy(f32[30,128,128]{2,1,0:T(8,128)} %pad_maximum_fusion) | data formatting | bytes 3932160 | tf_op jit(solution)/shard_map/concatenate | solution.py:58
  96.4 1.5 abs_reduce_fusion
  98.2 18.0 %while.12 = (s32[]{:T(128)}, f32[15,128,128]{1,2,0:T(8,128)S(1)}, f32[15,128,128]{2,1,0:T(8,128)S(1)}, s32[]{:T(128)}) while((s32[]{:T(128)}, f32[15,128,128]{1,2,0:T(8,128)S(1)}, f32[15,128,128]{2,1,0:T(8,128)S(1)}, s32[]{:T(128)}) %tuple.38), condition=%wide.region_7.8_spmd.clone, body=%wide.region_6.7_spmd.clone.sunk | while | flops 377765888 | bytes 7995445 | solution.py:30
  116.5 2.3 %collective-permute-start.2 = (f32[15,128,128]{2,1,0:T(8,128)S(1)}, f32[15,128,128]{2,1,0:T(8,128)S(1)}, u32[]{:S(2)}, u32[]{:S(2)}) collective-permute-start(f32[15,128,128]{2,1,0:T(8,128)S(1)} %copy.130), channel_id=1, source_target_pairs={{0,4},{4,0},{8,12},{12,8},{16,20},{20,16},{24,28},{28,24},{32,36},... | collective-permute-start | bytes 2949128 | tf_op jit(solution)/shard_map/ppermute | solution.py:108
  118.9 2.1 %collective-permute-done.2 = f32[15,128,128]{2,1,0:T(8,128)S(1)} collective-permute-done((f32[15,128,128]{2,1,0:T(8,128)S(1)}, f32[15,128,128]{2,1,0:T(8,128)S(1)}, u32[]{:S(2)}, u32[]{:S(2)}) %collective-permute-start.2) | collective-permute-done | bytes 983072 | tf_op jit(solution)/shard_map/ppermute | solution.py:108
  121.0 1.6 fusion.15
  129.9 5.2 %all-to-all-start.2 = ((bf16[64,2,400]{2,1,0:T(2,128)(2,1)}), bf16[64,2,400]{2,1,0:T(2,128)(2,1)S(1)}, u32[]{:S(2)}, u32[]{:S(2)}) async-start(bf16[64,2,400]{2,1,0:T(2,128)(2,1)} %reshape.127), calls=%async_computation.2 | async-start | bytes 262144 | tf_op jit(solution)/shard_map/all_to_all | solution.py:127
  135.8 10.8 %all-to-all-done.2 = bf16[64,2,400]{2,1,0:T(2,128)(2,1)S(1)} async-done(((bf16[64,2,400]{2,1,0:T(2,128)(2,1)}), bf16[64,2,400]{2,1,0:T(2,128)(2,1)S(1)}, u32[]{:S(2)}, u32[]{:S(2)}) %all-to-all-start.2) | async-done | bytes 102432 | tf_op jit(solution)/shard_map/all_to_all | solution.py:127
  148.9 5.5 %all_to_all.80 = bf16[2,1280,20]{1,0,2:T(2,128)(2,1)S(1)} all-to-all(bf16[2,1280,20]{1,0,2:T(2,128)(2,1)S(1)} %all_to_all.61), channel_id=1, replica_groups=mesh['y'=8,'z'=8,'core'=2,'tensor'=4] {'core'}, dimensions={2} | all-to-all | bytes 204800 | tf_op jit(solution)/shard_map/all_to_all | solution.py:128
  154.6 1.6 reshape.125
  156.9 1.4 reshape_reshape.3
  158.3 2.1 %convolution_convert_fusion = bf16[2,20,128,10]{2,3,1,0:T(8,128)(2,1)S(1)} fusion(bf16[2,20,128,128]{3,2,1,0:T(8,128)(2,1)} %all-gather.2.cloned.1.call-done, bf16[2,20,128,10]{2,1,3,0:T(8,128)(2,1)S(1)} %reshape_reshape.3), kind=kOutput, calls=%fused_computation.11 | convolution fusion | flops 13158400 | bytes 1515520 | tf_op jit(solution)/shard_map/lbij,lbjc->lbic/dot_general | solution.py:135
  160.4 1.6 convert_element_type.50
  162.1 3.6 %copy.155 = bf16[2,2,64,20,10]{4,0,3,2,1:T(2,128)(2,1)S(1)} copy(bf16[2,2,64,20,10]{3,1,2,4,0:T(2,128)(2,1)S(1)} %bitcast.106) | data formatting | bytes 204800 | tf_op jit(solution)/shard_map/reshape | solution.py:139
  165.7 2.4 %reshape.129 = bf16[2,2,12800]{2,1,0:T(2,128)(2,1)S(1)} reshape(bf16[2560,2,10]{2,1,0:T(2,128)(2,1)S(1)} %bitcast.96) | data formatting | bytes 204800
  168.1 3.9 %all_to_all.81 = bf16[2,2,12800]{2,1,0:T(2,128)(2,1)S(1)} all-to-all(bf16[2,2,12800]{2,1,0:T(2,128)(2,1)S(1)} %reshape.129), channel_id=1, replica_groups=mesh['y'=8,'z'=8,'core'=2,'tensor'=4] {'core'}, dimensions={0} | all-to-all | bytes 204800 | tf_op jit(solution)/shard_map/all_to_all | solution.py:142
  172.0 3.1 %reshape.130 = bf16[2560,2,10]{2,1,0:T(2,128)(2,1)S(1)} reshape(bf16[2,2,12800]{2,1,0:T(2,128)(2,1)S(1)} %all_to_all.81) | data formatting | bytes 204800
  177.8 4.6 %all-to-all-start.5 = ((bf16[64,2,400]{2,1,0:T(2,128)(2,1)}), bf16[64,2,400]{2,1,0:T(2,128)(2,1)S(1)}, u32[]{:S(2)}, u32[]{:S(2)}) async-start(bf16[64,2,400]{2,1,0:T(2,128)(2,1)} %reshape.131), calls=%async_computation.5 | async-start | bytes 262144 | tf_op jit(solution)/shard_map/all_to_all | solution.py:143
  183.4 2.1 %select_bitcast_fusion = f32[1,1,128,128]{3,2,1,0:T(8,128)} fusion(f32[30,128,128]{2,1,0:T(8,128)} %get-tuple-element.55, s32[]{:T(128)S(6)} %select_n.94, pred[]{:T(512)} %compare_reduce_fusion.1), kind=kLoop, calls=%fused_computation.34 | loop fusion | flops 16384 | bytes 131077 | tf_op jit(solution)/shard_map/broadcast_in_dim | solution.py:115
  185.5 8.6 %all-to-all-done.5 = bf16[64,2,400]{2,1,0:T(2,128)(2,1)S(1)} async-done(((bf16[64,2,400]{2,1,0:T(2,128)(2,1)}), bf16[64,2,400]{2,1,0:T(2,128)(2,1)S(1)}, u32[]{:S(2)}, u32[]{:S(2)}) %all-to-all-start.5) | async-done | bytes 102432 | tf_op jit(solution)/shard_map/all_to_all | solution.py:143
  195.1 1.9 all_to_all.72
  (100 shorter events, 40.5 us)
Async XLA Ops:
  18.0 10.3 %collective-permute-start = (f32[1024,128]{1,0:T(8,128)S(1)}, f32[1024,128]{1,0:T(8,128)S(1)}, u32[]{:S(2)}, u32[]{:S(2)}) collective-permute-start(f32[1024,128]{1,0:T(8,128)S(1)} %bitcast_select_fusion), channel_id=1, source_target_pairs={{0,4},{4,0},{1,5},{5,1},{2,6},{6,2},{3,7},{7,3},{8,12},{12,8},{9,1... | collective-permute-start | bytes 1572872 | tf_op jit(solution)/shard_map/ppermute | solution.py:69
  56.7 24.0 %all-to-all-start.1 = ((f32[64,16,128]{2,1,0:T(8,128)}), f32[64,16,128]{2,1,0:T(8,128)S(1)}, u32[]{:S(2)}, u32[]{:S(2)}) async-start(f32[64,16,128]{2,1,0:T(8,128)} %broadcast_in_dim.63), calls=%async_computation.1 | async-start | bytes 1048576 | tf_op jit(solution)/shard_map/all_to_all | solution.py:74
  64.4 93.9 %all-gather.2.cloned.1.call-start = ((), (), s32[]{:S(2)}) async-start(), calls=%async_computation.6 | async-start | bytes 1638400 | tf_op jit(solution)/shard_map/all_gather | solution.py:119
  80.7 7.2 %collective-permute-start.1 = (f32[1024,128]{1,0:T(8,128)S(1)}, f32[1024,128]{1,0:T(8,128)S(1)}, u32[]{:S(2)}, u32[]{:S(2)}) collective-permute-start(f32[1024,128]{1,0:T(8,128)S(1)} %bitcast.107), channel_id=1, source_target_pairs={{0,4},{4,0},{1,5},{5,1},{2,6},{6,2},{3,7},{7,3},{8,12},{12,8},{9,1... | collective-permute-start | bytes 1572872 | tf_op jit(solution)/shard_map/ppermute | solution.py:75
  88.0 1.0 copy-start
  116.5 4.5 %collective-permute-start.2 = (f32[15,128,128]{2,1,0:T(8,128)S(1)}, f32[15,128,128]{2,1,0:T(8,128)S(1)}, u32[]{:S(2)}, u32[]{:S(2)}) collective-permute-start(f32[15,128,128]{2,1,0:T(8,128)S(1)} %copy.130), channel_id=1, source_target_pairs={{0,4},{4,0},{8,12},{12,8},{16,20},{20,16},{24,28},{28,24},{32,36},... | collective-permute-start | bytes 2949128 | tf_op jit(solution)/shard_map/ppermute | solution.py:108
  118.8 4.6 %copy-start.4 = (s32[1,30]{1,0:T(1,128)S(1)}, s32[1,30]{1,0:T(1,128)}, u32[]{:S(2)}) copy-start(s32[1,30]{1,0:T(1,128)} %param.15) | copy-start | bytes 364
  118.9 6.5 %copy-start.2 = (bf16[2,20,1280]{2,0,1:T(2,128)(2,1)S(1)}, bf16[2,20,1280]{2,0,1:T(2,128)(2,1)}, u32[]{:S(2)}) copy-start(bf16[2,20,1280]{2,0,1:T(2,128)(2,1)} %param.12) | copy-start | bytes 307204
  127.9 7.2 %copy-start.3 = (s32[392]{0:T(512)S(1)}, s32[392]{0:T(512)}, u32[]{:S(2)}) copy-start(s32[392]{0:T(512)} %param.14) | copy-start | bytes 4708
  129.9 16.7 %all-to-all-start.2 = ((bf16[64,2,400]{2,1,0:T(2,128)(2,1)}), bf16[64,2,400]{2,1,0:T(2,128)(2,1)S(1)}, u32[]{:S(2)}, u32[]{:S(2)}) async-start(bf16[64,2,400]{2,1,0:T(2,128)(2,1)} %reshape.127), calls=%async_computation.2 | async-start | bytes 262144 | tf_op jit(solution)/shard_map/all_to_all | solution.py:127
  175.1 7.3 %copy-start.1 = (bf16[392,640]{1,0:T(8,128)(2,1)S(1)}, bf16[392,640]{1,0:T(8,128)(2,1)}, u32[]{:S(2)}) copy-start(bf16[392,640]{1,0:T(8,128)(2,1)} %param.13) | copy-start | bytes 1505284
  177.8 16.3 %all-to-all-start.5 = ((bf16[64,2,400]{2,1,0:T(2,128)(2,1)}), bf16[64,2,400]{2,1,0:T(2,128)(2,1)S(1)}, u32[]{:S(2)}, u32[]{:S(2)}) async-start(bf16[64,2,400]{2,1,0:T(2,128)(2,1)} %reshape.131), calls=%async_computation.5 | async-start | bytes 262144 | tf_op jit(solution)/shard_map/all_to_all | solution.py:143
Sparse Core Ops, SparseCore 0:
  123.5 22.2 all-gather.1

commit v8 on v6

--- a/solution.py
+++ b/solution.py
@@ -30,24 +30,35 @@
     return lax.fori_loop(0, NS_ITERS, sweep, approx)
 
 
-def pack_symmetric(blocks, count_part, fsdp_size):
+def pack_half(blocks, count_part, rows_out):
     half = BLK // 2
     rows = lax.broadcasted_iota(jnp.int32, (half, BLK), 0)
     lanes = lax.broadcasted_iota(jnp.int32, (half, BLK), 1)
     bottom = blocks[:, half:, :]
     panel = jnp.where(lanes >= rows, blocks[:, :half, :], jnp.roll(bottom, half, axis=2))
-    diag = jnp.sum(jnp.where(lanes == rows + half, bottom, 0.0), axis=2).reshape(-1, BLK)
+    diag = jnp.sum(jnp.where(lanes == rows + half, bottom, 0.0), axis=2).reshape(-1)
+    diag_rows = -(-diag.shape[0] // BLK)
+    diag = jnp.concatenate([diag, jnp.zeros((diag_rows * BLK - diag.shape[0],), jnp.float32)])
     count_row = jnp.zeros((1, BLK), jnp.float32).at[0, 0].set(count_part)
-    body = jnp.concatenate([panel.reshape(-1, BLK), diag, count_row], axis=0)
-    total = -(-body.shape[0] // fsdp_size) * fsdp_size
-    return jnp.concatenate([body, jnp.zeros((total - body.shape[0], BLK), jnp.float32)], axis=0)
+    body = jnp.concatenate([panel.reshape(-1, BLK), diag.reshape(diag_rows, BLK), count_row], axis=0)
+    return jnp.concatenate([body, jnp.zeros((rows_out - body.shape[0], BLK), jnp.float32)], axis=0)
+
+
+def pack_symmetric(blocks, count_part, fsdp_size):
+    share = blocks.shape[0] // 2
+    need = share * BLK // 2 + -(-share * BLK // 2 // BLK) + 1
+    rows_out = -(-need // (fsdp_size // 2)) * (fsdp_size // 2)
+    return jnp.concatenate(
+        [pack_half(blocks[:share], count_part, rows_out), pack_half(blocks[share:], count_part, rows_out)]
+    )
 
 
 def unpack_symmetric(summed, block_total):
     half = BLK // 2
     panel = summed[: block_total * half].reshape(block_total, half, BLK)
-    diag_rows = block_total * half // BLK
-    diag = summed[block_total * half : block_total * half + diag_rows].reshape(block_total, half)
+    diag_rows = -(-block_total * half // BLK)
+    diag = summed[block_total * half : block_total * half + diag_rows].reshape(-1)
+    diag = diag[: block_total * half].reshape(block_total, half)
     count_total = summed[block_total * half + diag_rows, 0]
     rows = lax.broadcasted_iota(jnp.int32, (half, BLK), 0)
     lanes = lax.broadcasted_iota(jnp.int32, (half, BLK), 1)
@@ -71,13 +82,7 @@
     pieces = lax.all_to_all(part.reshape(chips, chunk, BLK), CHIP_AXES, 0, 0, tiled=True)
     mine = jnp.sum(pieces, axis=0)
     spread = jnp.broadcast_to(mine[None], (chips, chunk, BLK))
-    own_half = lax.all_to_all(spread, CHIP_AXES, 0, 0, tiled=True).reshape(part.shape)
-    other_half = lax.ppermute(own_half, "core", [(0, 1), (1, 0)])
-    return jnp.where(
-        core == 0,
-        jnp.concatenate([own_half, other_half]),
-        jnp.concatenate([other_half, own_half]),
-    )
+    return lax.all_to_all(spread, CHIP_AXES, 0, 0, tiled=True).reshape(part.shape)
 
 
 def on_device(layer_inputs, out_grads, weight_grad, emb_grad, counts, owner_pos):
@@ -99,12 +104,11 @@
     count_part = jnp.sum(counts.astype(jnp.float32))
     packed = pack_symmetric(partials, count_part, fsdp_size)
     summed = sum_over_fsdp(packed, fsdp_size)
-    blocks_sum, count_total = unpack_symmetric(summed, block_total)
+    share = block_total // 2
+    blocks_sum, count_total = unpack_symmetric(summed, share)
     divisor = row_count * fsdp_size
-    factors = blocks_sum / divisor
     core = lax.axis_index(FSDP) % 2
-    share = block_total // 2
-    mine = newton_inverse(lax.dynamic_slice_in_dim(factors, core * share, share, axis=0))
+    mine = newton_inverse(blocks_sum / divisor)
     other = lax.ppermute(mine, FSDP, [(i, i ^ 1) for i in range(fsdp_size)])
     inv = jnp.where(core == 0, jnp.concatenate([mine, other]), jnp.concatenate([other, mine]))
     own_table = owner_pos[0]

time: 191 us -> 180 us (0.942)
  local copies, waits for them, and re-layouts: 25.7 us -> 22 us
  starting transfers between devices: 41.2 us -> 38.7 us
  other arithmetic: 14.9 us -> 12.5 us
  waiting for transfers between devices: 42 us -> 39.9 us
    ppermute x1 -> x0, starting transfers between devices: 5.65 us -> none  [sum_over_fsdp(): other_half = lax.ppermute(own_half, 'core', [(0, 1), (1, 0)])]
    ppermute x1, starting transfers between devices: 2.29 us -> 5.66 us  [on_device(): other = lax.ppermute(mine, FSDP, [(i, i ^ 1) for i in range(fsdp_size)])]
    concatenate x1, local copies, waits for them, and re-layouts: 2.83 us -> 0.33 us  [unpack_symmetric(): tri = jnp.concatenate([top, bottom], axis=1)]
    unnamed x17 -> x15, local copies, waits for them, and re-layouts: 10.7 us -> 9.9 us
  transfers between devices with their start and end apart: 7 -> 6, of which waited for: 6 -> 5; matrix products, arithmetic and copies ran while one was open for 6% -> 6% of each run, Pallas kernels for 0% -> 0%
where the time goes in v8:
time: 180 us; the launch traced here: 179 us
  waiting for transfers between devices  39.9 us (22%)
  starting transfers between devices  38.7 us (22%)
  blocking collectives  27.5 us (15%)
  local copies, waits for them, and re-layouts  22 us (12%)
  matrix products  20.7 us (12%)
  between operations  17.6 us (10%)
  other arithmetic  12.5 us (7%)
    all_to_all x1, blocking collectives, sum_over_fsdp(): lax.all_to_all(part.reshape(chips, chunk, BLK), CHIP_AXES, 0, 0, tiled=True)  27.5 us
    all_to_all x1, waiting for transfers between devices, sum_over_fsdp(): lax.all_to_all(spread, CHIP_AXES, 0, 0, tiled=True).reshape(part.shape)  15.5 us
    all_to_all x1, waiting for transfers between devices, on_device(): lax.all_to_all(right_done, FSDP, split_axis=2, concat_axis=1, tiled=True)  11.6 us
    all_to_all x1, starting transfers between devices, on_device(): lax.all_to_all(left_done, FSDP, split_axis=1, concat_axis=2, tiled=True)  10.5 us
    unnamed x15, local copies, waits for them, and re-layouts  9.9 us
    dot_general x8, matrix products, sweep(): jnp.einsum('bij,bjk->bik', damped, approx, precision=lax.Precision.HIGH)  9.18 us
    all_to_all x1, waiting for transfers between devices, on_device(): lax.all_to_all(left_done, FSDP, split_axis=1, concat_axis=2, tiled=True)  9.11 us
    ppermute x1, starting transfers between devices, sum_over_fsdp(): part = keep + lax.ppermute(send, 'core', [(0, 1), (1, 0)])  8.74 us
  transfers between devices with their start and end apart: 6, of which 5 were waited for; matrix products, arithmetic and copies ran while one was open for 6% of the time, Pallas kernels for 0%

profile of v8, /device:TPU:1, one launch (start us, length us, event | category | flops | bytes accessed | tf_op | source)
XLA Modules:
  0.0 179.3 jit_solution(11671959143717488675)
XLA Ops:
  7.8 2.8 %copy.87 = bf16[2,384,1280]{1,2,0:T(8,128)(2,1)S(1)} copy(bf16[2,384,1280]{2,1,0:T(8,128)(2,1)} %param.12) | data formatting | bytes 3932160 | tf_op args[0]
  11.6 1.6 copy.89
  17.3 8.7 %collective-permute-start = (f32[1024,128]{1,0:T(8,128)S(1)}, f32[1024,128]{1,0:T(8,128)S(1)}, u32[]{:S(2)}, u32[]{:S(2)}) collective-permute-start(f32[1024,128]{1,0:T(8,128)S(1)} %broadcast_select_fusion), channel_id=1, source_target_pairs={{0,4},{4,0},{1,5},{5,1},{2,6},{6,2},{3,7},{7,3},{8,12},{12,8},{9,1... | collective-permute-start | bytes 1572872 | tf_op jit(solution)/shard_map/ppermute | solution.py:80
  26.1 1.5 collective-permute-done
  27.8 27.5 %all_to_all.43 = f32[64,16,128]{2,1,0:T(8,128)S(1)} all-to-all(f32[64,16,128]{2,1,0:T(8,128)S(1)} %bitcast.87), channel_id=1, replica_groups=mesh['y'=8,'z'=8,'core'=2,'tensor'=4] {'y','z'}, dimensions={0} | all-to-all | bytes 1048576 | tf_op jit(solution)/shard_map/all_to_all | solution.py:82
  56.2 7.6 %all-to-all-start.1 = ((f32[64,16,128]{2,1,0:T(8,128)}), f32[64,16,128]{2,1,0:T(8,128)S(1)}, u32[]{:S(2)}, u32[]{:S(2)}) async-start(f32[64,16,128]{2,1,0:T(8,128)} %broadcast_in_dim.65), calls=%async_computation.1 | async-start | bytes 1048576 | tf_op jit(solution)/shard_map/all_to_all | solution.py:85
  64.7 15.5 %all-to-all-done.1 = f32[64,16,128]{2,1,0:T(8,128)S(1)} async-done(((f32[64,16,128]{2,1,0:T(8,128)}), f32[64,16,128]{2,1,0:T(8,128)S(1)}, u32[]{:S(2)}, u32[]{:S(2)}) %all-to-all-start.1) | async-done | bytes 524320 | tf_op jit(solution)/shard_map/all_to_all | solution.py:85
  83.1 1.0 broadcast_divide_fusion
  84.1 18.0 %while.13 = (s32[]{:T(128)}, f32[15,128,128]{1,2,0:T(8,128)S(1)}, f32[15,128,128]{2,1,0:T(8,128)S(1)}, s32[]{:T(128)}) while((s32[]{:T(128)}, f32[15,128,128]{1,2,0:T(8,128)S(1)}, f32[15,128,128]{2,1,0:T(8,128)S(1)}, s32[]{:T(128)}) %tuple.51), condition=%wide.region_8.9_spmd.clone, body=%wide.region_7.8_spmd.clone.sunk | while | flops 377765888 | bytes 7995445 | solution.py:30
  84.2 1.1 convolution_subtract_fusion.2
  86.4 1.1 convolution_subtract_fusion.2
  88.7 1.1 convolution_subtract_fusion.2
  90.9 1.1 convolution_subtract_fusion.2
  93.2 1.1 convolution_subtract_fusion.2
  95.4 1.1 convolution_subtract_fusion.2
  97.7 1.1 convolution_subtract_fusion.2
  99.9 1.1 convolution_subtract_fusion.2
  102.4 5.7 %collective-permute-start.1 = (f32[15,128,128]{2,1,0:T(8,128)S(1)}, f32[15,128,128]{2,1,0:T(8,128)S(1)}, u32[]{:S(2)}, u32[]{:S(2)}) collective-permute-start(f32[15,128,128]{2,1,0:T(8,128)S(1)} %copy.93), channel_id=1, source_target_pairs={{0,4},{4,0},{8,12},{12,8},{16,20},{20,16},{24,28},{28,24},{32,36},... | collective-permute-start | bytes 2949128 | tf_op jit(solution)/shard_map/ppermute | solution.py:112
  108.1 2.1 %collective-permute-done.1 = f32[15,128,128]{2,1,0:T(8,128)S(1)} collective-permute-done((f32[15,128,128]{2,1,0:T(8,128)S(1)}, f32[15,128,128]{2,1,0:T(8,128)S(1)}, u32[]{:S(2)}, u32[]{:S(2)}) %collective-permute-start.1) | collective-permute-done | bytes 983072 | tf_op jit(solution)/shard_map/ppermute | solution.py:112
  110.2 1.6 fusion.22
  118.2 1.2 reshape.151
  119.3 6.2 %all-to-all-start.2 = ((bf16[128,2,200]{2,1,0:T(2,128)(2,1)}), bf16[128,2,200]{2,1,0:T(2,128)(2,1)S(1)}, u32[]{:S(2)}, u32[]{:S(2)}) async-start(bf16[128,2,200]{2,1,0:T(2,128)(2,1)} %reshape.151), calls=%async_computation.2 | async-start | bytes 262144 | tf_op jit(solution)/shard_map/all_to_all | solution.py:130
  126.2 11.6 %all-to-all-done.2 = bf16[128,2,200]{2,1,0:T(2,128)(2,1)S(1)} async-done(((bf16[128,2,200]{2,1,0:T(2,128)(2,1)}), bf16[128,2,200]{2,1,0:T(2,128)(2,1)S(1)}, u32[]{:S(2)}, u32[]{:S(2)}) %all-to-all-start.2) | async-done | bytes 102432 | tf_op jit(solution)/shard_map/all_to_all | solution.py:130
  138.6 1.4 reshape.150
  140.0 2.1 %convolution_convert_fusion = bf16[2,20,128,10]{2,3,1,0:T(8,128)(2,1)S(1)} fusion(bf16[2,20,128,128]{3,2,1,0:T(8,128)(2,1)} %all-gather.2.cloned.1.call-done, bf16[2,20,128,10]{2,1,3,0:T(8,128)(2,1)S(1)} %reshape.150), kind=kOutput, calls=%fused_computation.9 | convolution fusion | flops 13158400 | bytes 1515520 | tf_op jit(solution)/shard_map/lbij,lbjc->lbic/dot_general | solution.py:133
  142.1 1.1 copy.111
  143.1 1.6 reshape.153
  144.8 10.5 %all-to-all-start.3 = ((bf16[128,2,200]{2,1,0:T(2,128)(2,1)}), bf16[128,2,200]{2,1,0:T(2,128)(2,1)S(1)}, u32[]{:S(2)}, u32[]{:S(2)}) async-start(bf16[128,2,200]{2,1,0:T(2,128)(2,1)} %reshape.153), calls=%async_computation.3 | async-start | bytes 262144 | tf_op jit(solution)/shard_map/all_to_all | solution.py:137
  156.2 2.1 %select_bitcast_fusion = f32[1,1,128,128]{3,2,1,0:T(8,128)} fusion(f32[30,128,128]{2,1,0:T(8,128)} %get-tuple-element.77, s32[]{:T(128)S(6)} %select_n.88, pred[]{:T(512)} %compare_reduce_fusion.1), kind=kLoop, calls=%fused_computation.43 | loop fusion | flops 16384 | bytes 131077 | tf_op jit(solution)/shard_map/broadcast_in_dim | solution.py:119
  158.3 9.1 %all-to-all-done.3 = bf16[128,2,200]{2,1,0:T(2,128)(2,1)S(1)} async-done(((bf16[128,2,200]{2,1,0:T(2,128)(2,1)}), bf16[128,2,200]{2,1,0:T(2,128)(2,1)S(1)}, u32[]{:S(2)}, u32[]{:S(2)}) %all-to-all-start.3) | async-done | bytes 102432 | tf_op jit(solution)/shard_map/all_to_all | solution.py:137
  168.4 2.3 %copy.112 = bf16[2,128,20,10]{2,1,0,3:T(8,128)(2,1)S(1)} copy(bf16[2,128,20,10]{3,0,2,1:T(2,128)(2,1)S(1)} %bitcast.78) | data formatting | bytes 204800 | tf_op jit(solution)/shard_map/all_to_all | solution.py:137
  171.4 1.1 copy.104
  (86 shorter events, 26.3 us)
Async XLA Ops:
  14.3 0.8 copy-start.1
  17.3 10.3 %collective-permute-start = (f32[1024,128]{1,0:T(8,128)S(1)}, f32[1024,128]{1,0:T(8,128)S(1)}, u32[]{:S(2)}, u32[]{:S(2)}) collective-permute-start(f32[1024,128]{1,0:T(8,128)S(1)} %broadcast_select_fusion), channel_id=1, source_target_pairs={{0,4},{4,0},{1,5},{5,1},{2,6},{6,2},{3,7},{7,3},{8,12},{12,8},{9,1... | collective-permute-start | bytes 1572872 | tf_op jit(solution)/shard_map/ppermute | solution.py:80
  56.2 24.0 %all-to-all-start.1 = ((f32[64,16,128]{2,1,0:T(8,128)}), f32[64,16,128]{2,1,0:T(8,128)S(1)}, u32[]{:S(2)}, u32[]{:S(2)}) async-start(f32[64,16,128]{2,1,0:T(8,128)} %broadcast_in_dim.65), calls=%async_computation.1 | async-start | bytes 1048576 | tf_op jit(solution)/shard_map/all_to_all | solution.py:85
  63.8 76.1 %all-gather.2.cloned.1.call-start = ((), (), s32[]{:S(2)}) async-start(), calls=%async_computation.4 | async-start | bytes 1638400 | tf_op jit(solution)/shard_map/all_gather | solution.py:123
  102.4 7.8 %collective-permute-start.1 = (f32[15,128,128]{2,1,0:T(8,128)S(1)}, f32[15,128,128]{2,1,0:T(8,128)S(1)}, u32[]{:S(2)}, u32[]{:S(2)}) collective-permute-start(f32[15,128,128]{2,1,0:T(8,128)S(1)} %copy.93), channel_id=1, source_target_pairs={{0,4},{4,0},{8,12},{12,8},{16,20},{20,16},{24,28},{28,24},{32,36},... | collective-permute-start | bytes 2949128 | tf_op jit(solution)/shard_map/ppermute | solution.py:112
  108.1 5.5 %copy-start.3 = (s32[1,30]{1,0:T(1,128)S(1)}, s32[1,30]{1,0:T(1,128)}, u32[]{:S(2)}) copy-start(s32[1,30]{1,0:T(1,128)} %param.17) | copy-start | bytes 364
  117.3 8.2 %copy-start.2 = (s32[392]{0:T(512)S(1)}, s32[392]{0:T(512)}, u32[]{:S(2)}) copy-start(s32[392]{0:T(512)} %param.16) | copy-start | bytes 4708
  119.3 18.5 %all-to-all-start.2 = ((bf16[128,2,200]{2,1,0:T(2,128)(2,1)}), bf16[128,2,200]{2,1,0:T(2,128)(2,1)S(1)}, u32[]{:S(2)}, u32[]{:S(2)}) async-start(bf16[128,2,200]{2,1,0:T(2,128)(2,1)} %reshape.151), calls=%async_computation.2 | async-start | bytes 262144 | tf_op jit(solution)/shard_map/all_to_all | solution.py:130
  142.1 13.2 %copy-start = (bf16[392,640]{1,0:T(8,128)(2,1)S(1)}, bf16[392,640]{1,0:T(8,128)(2,1)}, u32[]{:S(2)}) copy-start(bf16[392,640]{1,0:T(8,128)(2,1)} %param.15) | copy-start | bytes 1505284
  144.8 22.7 %all-to-all-start.3 = ((bf16[128,2,200]{2,1,0:T(2,128)(2,1)}), bf16[128,2,200]{2,1,0:T(2,128)(2,1)S(1)}, u32[]{:S(2)}, u32[]{:S(2)}) async-start(bf16[128,2,200]{2,1,0:T(2,128)(2,1)} %reshape.153), calls=%async_computation.3 | async-start | bytes 262144 | tf_op jit(solution)/shard_map/all_to_all | solution.py:137
Sparse Core Ops, SparseCore 0:
  112.7 22.2 all-gather.1
